TPU v7x, 128 devices: a whole 4x4x4 slice. The times are simulated.
128 devices in a mesh: row: 64 (over y, x, z_lo, core), col: 2 (over z_hi).
Axes of the slice: x: 4, y: 4, z: 4 (z_hi: 2, z_lo: 2; z = z_hi * 2 + z_lo), core: 2. Of those that a mesh axis runs over, the one named last changes fastest.
Arguments:
- dist_first: bfloat16 [32768, 32768], P('row', 'col'), may hold values from -0.34 to 0.34
- coupling: bfloat16 [32768, 256], P('row', 'col'), may hold values from 0.099609375 to 1
- dist_second: bfloat16 [256, 512], P(None, 'col'), may hold values from -12 to 12
- row_potential: float32 [32768], P('row'), may hold values from -150 to 120
- column_cost: float32 [512], P('col'), may hold values from -300 to 20
- column_mass: float32 [512], P('col'), may hold values from 0.5 to 2
Outputs:
- transport: bfloat16 [32768, 512], P('row', 'col')
- potential: float32 [512], P('col')
All inputs are finite; a program needn't handle non-finite values.
Results may differ from a plain program's by a relative error of at most 0.0051.
Values may be sent and summed in bfloat16 or wider, within the bound.
No kernel may reach another device: no remote copies, remote signals or barrier semaphores. Data moves between devices by JAX's collectives and lax.ppermute only.
A program may use at most 128 MiB of HBM per device.

v0:
```python
import jax
import jax.numpy as jnp
from jax import lax
from jax.sharding import PartitionSpec as P

N = 32768


def joined_along(blocks, dim):
    shape = list(blocks.shape[1:])
    shape[dim] *= blocks.shape[0]
    return jnp.moveaxis(blocks, 0, dim).reshape(shape)


def copy_for_each(array, axis):
    copies = jnp.broadcast_to(array, (lax.axis_size(axis), *array.shape))
    return lax.all_to_all(copies, axis, split_axis=0, concat_axis=0, tiled=True)


def gather_directly(array, axis, dim):
    return joined_along(copy_for_each(array, axis), dim)


def split_up(array, dim, length):
    shape = array.shape
    blocks = array.reshape(*shape[:dim], length, shape[dim] // length, *shape[dim + 1 :])
    return jnp.moveaxis(blocks, dim, 0)


def summed_on_arrival(array, axis, dim):
    length = lax.axis_size(axis)
    blocks = lax.all_to_all(split_up(array, dim, length), axis, 0, 0, tiled=True)
    return jnp.sum(blocks, axis=0)


def all_in_one(array, axis):
    leaves = jax.tree.leaves(array)
    sequence = sorted(range(len(leaves)), key=lambda k: -leaves[k].size)
    width = (1, *leaves[sequence[0]].shape)[-1]
    lines = [
        jnp.pad(leaves[k].reshape(-1), (0, -leaves[k].size % width)).reshape(-1, width)
        for k in sequence
    ]
    both, at, found = (copy_for_each(jnp.concatenate(lines), axis), 0, {})
    for k, line in zip(sequence, lines):
        section = both[:, at : at + len(line)].reshape(len(both), -1)
        found[k] = section[:, : leaves[k].size].reshape(-1, *leaves[k].shape)
        at += len(line)
    numbers = iter(range(len(leaves)))
    return jax.tree.map(lambda _: found[next(numbers)], array)


def combined_pairwise(pieces, combine):
    while len(jax.tree.leaves(pieces)[0]) > 1:
        pieces = jax.vmap(combine)(
            *(jax.tree.map(lambda part: part[side::2], pieces) for side in (0, 1))
        )
    return jax.tree.map(lambda part: part[0], pieces)


def merged(array, axis, combine):
    pieces = all_in_one(array, axis)
    return combined_pairwise(pieces, combine)


def merge_columns(earlier, later):
    highest = jnp.maximum(earlier[0], later[0])
    summed = earlier[1] * jnp.exp(earlier[0] - highest) + later[1] * jnp.exp(later[0] - highest)
    return (highest, summed)


def body(dist_first, coupling, dist_second, row_potential, column_cost, column_mass):
    groups = lax.axis_size("col")
    stacked = lax.all_gather(coupling, "row", axis=0, tiled=True)
    total_rows = stacked.shape[0]
    stacked = stacked.reshape(groups, 1, total_rows // groups, stacked.shape[1])
    traded = lax.all_to_all(stacked, "col", split_axis=0, concat_axis=1, tiled=True)
    second_full = gather_directly(dist_second, "col", 1)
    second_blocks = second_full.reshape(
        groups, second_full.shape[0] // groups, second_full.shape[1]
    )
    product = jnp.einsum(
        "jnk,jkq->nq", traded[0], second_blocks, preferred_element_type=jnp.float32
    ).astype(jnp.bfloat16)
    partial_value = jnp.dot(dist_first, product, preferred_element_type=jnp.float32)
    gradient = summed_on_arrival(partial_value, "col", 1)
    scores = row_potential[:, None] + 2.0 * gradient - column_cost[None, :]
    local_high = jnp.max(scores, axis=0)
    local_sum = jnp.sum(jnp.exp(scores - local_high[None, :]), axis=0)
    highest, column_sum = merged((local_high, local_sum), "row", merge_columns)
    weights = jnp.exp(scores - highest[None, :])
    potential = jnp.log(column_mass) - highest - jnp.log(column_sum)
    transport = (weights * (N * column_mass / column_sum)[None, :]).astype(jnp.bfloat16)
    return (transport, potential)


def solution(mesh):
    in_specs = (P("row", "col"), P("row", "col"), P(None, "col"), P("row"), P("col"), P("col"))
    out_specs = (P("row", "col"), P("col"))
    return jax.shard_map(body, mesh=mesh, in_specs=in_specs, out_specs=out_specs, check_vma=False)
```

profile of v0, /device:TPU:1, one launch (start us, length us, event | category | flops | bytes accessed | tf_op | source)
XLA Modules:
  0.0 284.0 jit_solution(13788722296052831946)
XLA Ops:
  7.2 0.0 all-gather.2.cloned.1.call-start
  7.2 0.7 all-gather.2.cloned.1.call-update
  7.9 0.9 broadcast_in_dim.4
  8.8 11.0 %all_to_all.24 = bf16[2,256,256]{2,1,0:T(8,128)(2,1)S(1)} all-to-all(bf16[2,256,256]{2,1,0:T(8,128)(2,1)S(1)} %broadcast_in_dim.4), channel_id=1, replica_groups=mesh['row'=64,'col'=2] {'col'}, dimensions={0} | all-to-all | bytes 524288 | tf_op jit(solution)/shard_map/all_to_all | solution.py:17
  19.8 104.5 %all-gather.2.cloned.1.call-done = bf16[32768,128]{1,0:T(8,128)(2,1)} async-done(((bf16[512,128]{1,0:T(8,128)(2,1)}), bf16[32768,128]{1,0:T(8,128)(2,1)}) %all-gather.2.cloned.1.call-update) | async-done | bytes 8388624 | tf_op jit(solution)/shard_map/all_gather | solution.py:74
  124.4 6.9 %all-to-all-start = ((bf16[2,1,16384,128]{3,2,1,0:T(8,128)(2,1)}), bf16[2,1,16384,128]{3,2,1,0:T(8,128)(2,1)}, u32[]{:S(2)}, u32[]{:S(2)}) async-start(bf16[2,1,16384,128]{3,2,1,0:T(8,128)(2,1)} %bitcast.26), calls=%async_computation | async-start | bytes 16777216 | tf_op jit(solution)/shard_map/all_to_all | solution.py:77
  131.3 0.3 copy.10
  131.6 0.2 reshape_reshape.3
  131.8 0.0 copy-start
  131.8 0.0 copy-start.1
  131.8 0.0 copy-start.2
  131.8 93.2 %all-to-all-done = bf16[2,1,16384,128]{3,2,1,0:T(8,128)(2,1)} async-done(((bf16[2,1,16384,128]{3,2,1,0:T(8,128)(2,1)}), bf16[2,1,16384,128]{3,2,1,0:T(8,128)(2,1)}, u32[]{:S(2)}, u32[]{:S(2)}) %all-to-all-start) | async-done | bytes 8388640 | tf_op jit(solution)/shard_map/all_to_all | solution.py:77
  225.0 16.6 %fusion.2 = f32[512,512]{1,0:T(8,128)S(1)} fusion(bf16[512,16384]{1,0:T(8,128)(2,1)} %param.6, bf16[2,128,512]{2,1,0:T(8,128)(2,1)S(1)} %reshape_reshape.3, bf16[2,1,16384,128]{3,2,1,0:T(8,128)(2,1)} %all-to-all-done), kind=kOutput, calls=%fused_computation.2 | convolution fusion | flops 12893290496 | bytes 26476544 | tf_op jit(solution)/shard_map/dot_general | solution.py:85
  241.6 16.5 %all_to_all.25 = f32[2,512,256]{1,2,0:T(8,128)S(1)} all-to-all(f32[2,512,256]{1,2,0:T(8,128)S(1)} %bitcast.27), channel_id=1, replica_groups=mesh['row'=64,'col'=2] {'col'}, dimensions={0} | all-to-all | bytes 2097152 | tf_op jit(solution)/shard_map/all_to_all | solution.py:32
  258.1 0.1 reduce_sum.18
  258.2 0.0 copy-done
  258.2 0.0 copy-done.1
  258.2 0.2 fusion.4
  258.4 0.2 exponential_reduce_fusion
  258.7 16.2 %all_to_all.26 = f32[64,2,256]{2,1,0:T(2,128)S(1)} all-to-all(f32[64,2,256]{2,1,0:T(2,128)S(1)} %broadcast_in_dim.5), channel_id=1, replica_groups=mesh['row'=64,'col'=2] {'row'}, dimensions={0} | all-to-all | bytes 262144 | tf_op jit(solution)/shard_map/all_to_all | solution.py:17
  274.9 0.1 fusion.6
  275.6 0.0 copy-done.2
  275.6 0.6 log_subtract_fusion
  276.2 0.2 multiply_convert_fusion
  276.4 0.8 copy.12
  (29 shorter events, 0.5 us)
Async XLA Ops:
  7.2 117.2 %all-gather.2.cloned.1.call-start = ((), (), s32[]{:S(2)}) async-start(), calls=%async_computation.4 | async-start | bytes 8519680 | tf_op jit(solution)/shard_map/all_gather | solution.py:74
  124.4 100.6 %all-to-all-start = ((bf16[2,1,16384,128]{3,2,1,0:T(8,128)(2,1)}), bf16[2,1,16384,128]{3,2,1,0:T(8,128)(2,1)}, u32[]{:S(2)}, u32[]{:S(2)}) async-start(bf16[2,1,16384,128]{3,2,1,0:T(8,128)(2,1)} %bitcast.26), calls=%async_computation | async-start | bytes 16777216 | tf_op jit(solution)/shard_map/all_to_all | solution.py:77
  131.8 126.4 %copy-start = (f32[512]{0:T(512)S(1)}, f32[512]{0:T(512)}, u32[]{:S(2)}) copy-start(f32[512]{0:T(512)} %param.9) | copy-start | bytes 6148
  131.8 126.4 %copy-start.1 = (f32[256]{0:T(256)S(1)}, f32[256]{0:T(256)}, u32[]{:S(2)}) copy-start(f32[256]{0:T(256)} %param.10) | copy-start | bytes 3076
  131.8 143.8 %copy-start.2 = (f32[256]{0:T(256)S(1)}, f32[256]{0:T(256)}, u32[]{:S(2)}) copy-start(f32[256]{0:T(256)} %param.11) | copy-start | bytes 3076
Sparse Core Ops, SparseCore 0:
  9.7 114.6 all-gather.1
where the time goes:
time: 284 us
  waiting for transfers between devices  198 us (70%)
  blocking collectives  43.7 us (15%)
  matrix products  16.6 us (6%)
  between operations  14.2 us (5%)
  starting transfers between devices  6.97 us (2%)
    all_gather x1, waiting for transfers between devices, body(): stacked = lax.all_gather(coupling, 'row', axis=0, tiled=True)  105 us
    all_to_all x1, waiting for transfers between devices, body(): lax.all_to_all(stacked, 'col', split_axis=0, concat_axis=1, tiled=True)  93.2 us
    all_to_all x2, blocking collectives, copy_for_each(): return lax.all_to_all(copies, axis, split_axis=0, concat_axis=0, tiled=True)  27.2 us
    dot_general x1, matrix products, body(): jnp.dot(dist_first, product, preferred_element_type=jnp.float32)  16.6 us
    all_to_all x1, blocking collectives, summed_on_arrival(): lax.all_to_all(split_up(array, dim, length), axis, 0, 0, tiled=True)  16.5 us
    all_to_all x1, starting transfers between devices, body(): lax.all_to_all(stacked, 'col', split_axis=0, concat_axis=1, tiled=True)  6.93 us
  transfers between devices with their start and end apart: 2, of which 2 were waited for; matrix products, arithmetic and copies ran while one was open for 0% of the time, Pallas kernels for 0%

commit v1 on v0

v1 whole, which is shorter than its diff:
```python
import jax
import jax.numpy as jnp
import numpy as np
from jax import lax
from jax.sharding import Mesh
from jax.sharding import PartitionSpec as P

N = 32768
AXES = ("yh", "yl", "x", "zl", "core", "zh")
ROWS = ("yh", "yl", "x", "zl", "core")
GATHER = ("yl", "x", "zl", "core")


def body(dist_first, coupling, dist_second, row_potential, column_cost, column_mass):
    zh = lax.axis_index("zh")
    yh = lax.axis_index("yh")
    blocks = coupling.shape[0]
    k_half = coupling.shape[1]
    q_half = dist_second.shape[1]

    coupling_x = lax.ppermute(coupling, "zh", [(0, 1), (1, 0)])
    second_x = lax.ppermute(dist_second, "zh", [(0, 1), (1, 0)])

    piece = jnp.concatenate([coupling, coupling_x], axis=1)
    into_other_half = [(0, 4), (2, 6), (5, 1), (7, 3)]
    moved = lax.ppermute(piece, ("yh", "yl", "zh"), into_other_half)
    piece = jnp.where(yh == zh, piece, moved)

    gathered = lax.all_gather(piece, GATHER, axis=0, tiled=True)

    second_full = jnp.concatenate([dist_second, second_x], axis=1)
    second_k = jnp.concatenate(
        [
            lax.dynamic_slice_in_dim(second_full, zh * k_half, k_half, axis=0),
            lax.dynamic_slice_in_dim(second_full, (1 - zh) * k_half, k_half, axis=0),
        ]
    )

    def partial_gradient(cols):
        product = jnp.dot(
            gathered, second_k[:, cols], preferred_element_type=jnp.float32
        ).astype(jnp.bfloat16)
        return jnp.dot(dist_first, product, preferred_element_type=jnp.float32)

    other_part = partial_gradient(slice(q_half, 2 * q_half))
    arrived = lax.ppermute(other_part, "zh", [(0, 1), (1, 0)])
    own_part = partial_gradient(slice(0, q_half))
    own_part, arrived = lax.optimization_barrier((own_part, arrived))
    gradient = own_part + arrived

    scores = row_potential[:, None] + 2.0 * gradient - column_cost[None, :]
    local_high = jnp.max(scores, axis=0)
    local_sum = jnp.sum(jnp.exp(scores - local_high[None, :]), axis=0)
    stats = lax.all_gather(jnp.stack([local_high, local_sum]), ROWS, axis=0, tiled=False)
    highest = jnp.max(stats[:, 0], axis=0)
    column_sum = jnp.sum(stats[:, 1] * jnp.exp(stats[:, 0] - highest[None, :]), axis=0)
    weights = jnp.exp(scores - highest[None, :])
    potential = jnp.log(column_mass) - highest - jnp.log(column_sum)
    transport = (weights * (N * column_mass / column_sum)[None, :]).astype(jnp.bfloat16)
    return (transport, potential)


def solution(mesh):
    devices = np.asarray(mesh.devices).reshape(2, 2, 4, 2, 2, 2)
    fine = Mesh(devices, AXES)
    in_specs = (P(ROWS, "zh"), P(ROWS, "zh"), P(None, "zh"), P(ROWS), P("zh"), P("zh"))
    out_specs = (P(ROWS, "zh"), P("zh"))
    return jax.shard_map(body, mesh=fine, in_specs=in_specs, out_specs=out_specs, check_vma=False)
```

time: 284 us -> 211 us (0.74)
  waiting for transfers between devices: 198 us -> 72.1 us
  blocking collectives: 43.7 us -> 80.9 us
  starting transfers between devices: 6.97 us -> 15.1 us
  matrix products: 16.6 us -> 23.4 us
    all_to_all x1 -> x0, waiting for transfers between devices: 93.2 us -> none  [body(): lax.all_to_all(stacked, 'col', split_axis=0, concat_axis=1, tiled=True)]
    all_gather x0 -> x1, blocking collectives: none -> 80.9 us  [body(): lax.all_gather(jnp.stack([local_high, local_sum]), ROWS, axis=0, tiled=Fa...]
    all_to_all x3 -> x0, blocking collectives: 43.7 us -> none  [the longest x2 27.2 us: copy_for_each(): return lax.all_to_all(copies, axis, split_axis=0, concat_axis=0, tiled=True)]
    all_gather x1, waiting for transfers between devices: 105 us -> 63 us  [body(): gathered = lax.all_gather(piece, GATHER, axis=0, tiled=True)]
    ppermute x0 -> x4, starting transfers between devices: none -> 15 us  [the longest x1 4.83 us: body(): moved = lax.ppermute(piece, ('yh', 'yl', 'zh'), into_other_half)]
    ppermute x0 -> x4, waiting for transfers between devices: none -> 9.06 us  [the longest x1 4.33 us: body(): moved = lax.ppermute(piece, ('yh', 'yl', 'zh'), into_other_half)]
    all_to_all x1 -> x0, starting transfers between devices: 6.93 us -> none  [body(): lax.all_to_all(stacked, 'col', split_axis=0, concat_axis=1, tiled=True)]
    dot_general x1 -> x2, matrix products: 16.6 us -> 23.4 us  [partial_gradient(): return jnp.dot(dist_first, product, preferred_element_type=jnp.float32)]
  transfers between devices with their start and end apart: 2 -> 5, of which waited for: 2 -> 5; matrix products, arithmetic and copies ran while one was open for 0% -> 6% of each run, Pallas kernels for 0% -> 0%
where the time goes in v1:
time: 211 us; the launch traced here: 210 us
  blocking collectives  80.9 us (38%)
  waiting for transfers between devices  72.1 us (34%)
  matrix products  23.4 us (11%)
  starting transfers between devices  15.1 us (7%)
  between operations  14.1 us (7%)
  local copies, waits for them, and re-layouts  2.84 us (1%)
    all_gather x1, blocking collectives, body(): lax.all_gather(jnp.stack([local_high, local_sum]), ROWS, axis=0, tiled=Fa...  80.9 us
    all_gather x1, waiting for transfers between devices, body(): gathered = lax.all_gather(piece, GATHER, axis=0, tiled=True)  63 us
    dot_general x2, matrix products, partial_gradient(): return jnp.dot(dist_first, product, preferred_element_type=jnp.float32)  23.4 us
    ppermute x1, starting transfers between devices, body(): moved = lax.ppermute(piece, ('yh', 'yl', 'zh'), into_other_half)  4.83 us
    ppermute x1, starting transfers between devices, body(): coupling_x = lax.ppermute(coupling, 'zh', [(0, 1), (1, 0)])  4.51 us
    ppermute x1, waiting for transfers between devices, body(): moved = lax.ppermute(piece, ('yh', 'yl', 'zh'), into_other_half)  4.33 us
  transfers between devices with their start and end apart: 5, of which 5 were waited for; matrix products, arithmetic and copies ran while one was open for 6% of the time, Pallas kernels for 0%

profile of v1, /device:TPU:1, one launch (start us, length us, event | category | flops | bytes accessed | tf_op | source)
XLA Modules:
  0.0 210.5 jit_solution(4188174330190762667)
XLA Ops:
  7.2 0.0 all-gather.4.cloned.1.call-start
  7.2 4.5 %collective-permute-start = (bf16[512,128]{1,0:T(8,128)(2,1)}, bf16[512,128]{1,0:T(8,128)(2,1)S(1)}, u32[]{:S(2)}, u32[]{:S(2)}) collective-permute-start(bf16[512,128]{1,0:T(8,128)(2,1)} %param.7), channel_id=1, source_target_pairs={{0,1},{1,0},{2,3},{3,2},{4,5},{5,4},{6,7},{7,6},{8,9},{9,8},{10,11... | collective-permute-start | bytes 393224 | tf_op jit(solution)/shard_map/ppermute | solution.py:21
  11.7 1.0 constant_dynamic-update-slice_fusion.1
  12.7 2.5 %collective-permute-done = bf16[512,128]{1,0:T(8,128)(2,1)S(1)} collective-permute-done((bf16[512,128]{1,0:T(8,128)(2,1)}, bf16[512,128]{1,0:T(8,128)(2,1)S(1)}, u32[]{:S(2)}, u32[]{:S(2)}) %collective-permute-start) | collective-permute-done | bytes 131104 | tf_op jit(solution)/shard_map/ppermute | solution.py:21
  15.2 4.8 %collective-permute-start.1 = (bf16[512,256]{1,0:T(8,128)(2,1)S(1)}, bf16[512,256]{1,0:T(8,128)(2,1)S(1)}, u32[]{:S(2)}, u32[]{:S(2)}) collective-permute-start(bf16[512,256]{1,0:T(8,128)(2,1)S(1)} %constant_dynamic-update-slice_fusion), channel_id=1, source_target_pairs={{0,64},{32,96},{65,1},{97,33},{2,66},{34,98},{67,3},{99,35},{4,68}... | collective-permute-start | bytes 786440 | tf_op jit(solution)/shard_map/ppermute | solution.py:26
  20.0 4.3 %collective-permute-done.1 = bf16[512,256]{1,0:T(8,128)(2,1)S(1)} collective-permute-done((bf16[512,256]{1,0:T(8,128)(2,1)S(1)}, bf16[512,256]{1,0:T(8,128)(2,1)S(1)}, u32[]{:S(2)}, u32[]{:S(2)}) %collective-permute-start.1) | collective-permute-done | bytes 262176 | tf_op jit(solution)/shard_map/ppermute | solution.py:26
  24.4 0.7 broadcast_select_fusion
  25.1 0.0 all-gather.4.cloned.1.call-update
  25.1 3.2 %collective-permute-start.2 = (bf16[256,256]{1,0:T(8,128)(2,1)}, bf16[256,256]{1,0:T(8,128)(2,1)S(1)}, u32[]{:S(2)}, u32[]{:S(2)}) collective-permute-start(bf16[256,256]{1,0:T(8,128)(2,1)} %param.8), channel_id=1, source_target_pairs={{0,1},{1,0},{2,3},{3,2},{4,5},{5,4},{6,7},{7,6},{8,9},{9,8},{10,11... | collective-permute-start | bytes 393224 | tf_op jit(solution)/shard_map/ppermute | solution.py:22
  28.3 0.9 constant_dynamic-update-slice_fusion.3
  29.3 1.6 collective-permute-done.2
  30.9 63.0 %all-gather.4.cloned.1.call-done = bf16[16384,256]{1,0:T(8,128)(2,1)} async-done(((bf16[512,256]{1,0:T(8,128)(2,1)}), bf16[16384,256]{1,0:T(8,128)(2,1)}) %all-gather.4.cloned.1.call-update) | async-done | bytes 8388624 | tf_op jit(solution)/shard_map/all_gather | solution.py:29
  93.9 11.7 %fusion.2 = f32[512,256]{0,1:T(8,128)S(1)} fusion(bf16[512,16384]{1,0:T(8,128)(2,1)} %param.6, bf16[16384,256]{1,0:T(8,128)(2,1)} %all-gather.4.cloned.1.call-done, bf16[128,512]{1,0:T(8,128)(2,1)S(1)} %get-tuple-element.12, bf16[128,512]{1,0:T(8,128)(2,1)S(1)} %get-tuple-element.13), kind=kOutput, calls=%fused_computation.4 | convolution fusion | flops 6446907392 | bytes 25952256 | tf_op jit(solution)/shard_map/dot_general | solution.py:43
  105.6 0.0 copy-start
  105.6 0.0 copy-start.1
  105.7 0.0 copy-start.2
  105.7 2.5 %collective-permute-start.3 = (f32[512,256]{0,1:T(8,128)S(1)}, f32[512,256]{0,1:T(8,128)S(1)}, u32[]{:S(2)}, u32[]{:S(2)}) collective-permute-start(f32[512,256]{0,1:T(8,128)S(1)} %fusion.2), channel_id=1, source_target_pairs={{0,1},{1,0},{2,3},{3,2},{4,5},{5,4},{6,7},{7,6},{8,9},{9,8},{10,11... | collective-permute-start | bytes 1572872 | tf_op jit(solution)/shard_map/ppermute | solution.py:46
  108.2 11.7 %fusion.3 = f32[512,256]{0,1:T(8,128)S(1)} fusion(bf16[512,16384]{1,0:T(8,128)(2,1)} %param.6, bf16[16384,256]{1,0:T(8,128)(2,1)} %all-gather.4.cloned.1.call-done, bf16[128,512]{1,0:T(8,128)(2,1)S(1)} %get-tuple-element.13, bf16[128,512]{1,0:T(8,128)(2,1)S(1)} %get-tuple-element.12), kind=kOutput, calls=%fused_computation.5 | convolution fusion | flops 6446907392 | bytes 25952256 | tf_op jit(solution)/shard_map/dot_general | solution.py:43
  119.9 0.6 collective-permute-done.3
  120.5 0.0 copy-done
  120.5 0.0 copy-done.1
  120.5 0.2 fusion.16
  120.7 0.2 exponential_reduce_fusion
  120.9 80.9 %all-gather.1 = f32[64,2,256]{2,1,0:T(2,128)S(1)} all-gather(f32[1,2,256]{2,1,0:T(2,128)S(1)} %maximum_bitcast_fusion), channel_id=2, replica_groups=mesh['yh'=2,'yl'=2,'x'=4,'zl'=2,'core'=2,'zh'=2] {'yh','yl','x','zl','co..., dimensions={0}, use_global_device_ids=true | all-gather | bytes 133120 | tf_op jit(solution)/shard_map/all_gather | solution.py:54
  201.9 0.1 slice_reduce_fusion
  202.1 0.0 copy-done.2
  202.1 0.6 log_subtract_fusion
  202.6 0.1 multiply_convert_fusion
  202.8 0.8 copy.11
  (5 shorter events, 0.1 us)
Async XLA Ops:
  7.2 86.8 %all-gather.4.cloned.1.call-start = ((), (), s32[]{:S(2)}) async-start(), calls=%async_computation | async-start | bytes 8650752 | tf_op jit(solution)/shard_map/all_gather | solution.py:29
  7.2 7.9 %collective-permute-start = (bf16[512,128]{1,0:T(8,128)(2,1)}, bf16[512,128]{1,0:T(8,128)(2,1)S(1)}, u32[]{:S(2)}, u32[]{:S(2)}) collective-permute-start(bf16[512,128]{1,0:T(8,128)(2,1)} %param.7), channel_id=1, source_target_pairs={{0,1},{1,0},{2,3},{3,2},{4,5},{5,4},{6,7},{7,6},{8,9},{9,8},{10,11... | collective-permute-start | bytes 393224 | tf_op jit(solution)/shard_map/ppermute | solution.py:21
  15.2 9.2 %collective-permute-start.1 = (bf16[512,256]{1,0:T(8,128)(2,1)S(1)}, bf16[512,256]{1,0:T(8,128)(2,1)S(1)}, u32[]{:S(2)}, u32[]{:S(2)}) collective-permute-start(bf16[512,256]{1,0:T(8,128)(2,1)S(1)} %constant_dynamic-update-slice_fusion), channel_id=1, source_target_pairs={{0,64},{32,96},{65,1},{97,33},{2,66},{34,98},{67,3},{99,35},{4,68}... | collective-permute-start | bytes 786440 | tf_op jit(solution)/shard_map/ppermute | solution.py:26
  25.1 5.8 %collective-permute-start.2 = (bf16[256,256]{1,0:T(8,128)(2,1)}, bf16[256,256]{1,0:T(8,128)(2,1)S(1)}, u32[]{:S(2)}, u32[]{:S(2)}) collective-permute-start(bf16[256,256]{1,0:T(8,128)(2,1)} %param.8), channel_id=1, source_target_pairs={{0,1},{1,0},{2,3},{3,2},{4,5},{5,4},{6,7},{7,6},{8,9},{9,8},{10,11... | collective-permute-start | bytes 393224 | tf_op jit(solution)/shard_map/ppermute | solution.py:22
  105.6 14.9 %copy-start = (f32[512]{0:T(512)S(1)}, f32[512]{0:T(512)}, u32[]{:S(2)}) copy-start(f32[512]{0:T(512)} %param.9) | copy-start | bytes 6148
  105.6 14.9 %copy-start.1 = (f32[256]{0:T(256)S(1)}, f32[256]{0:T(256)}, u32[]{:S(2)}) copy-start(f32[256]{0:T(256)} %param.10) | copy-start | bytes 3076
  105.7 96.4 %copy-start.2 = (f32[256]{0:T(256)S(1)}, f32[256]{0:T(256)}, u32[]{:S(2)}) copy-start(f32[256]{0:T(256)} %param.11) | copy-start | bytes 3076
  105.7 14.8 %collective-permute-start.3 = (f32[512,256]{0,1:T(8,128)S(1)}, f32[512,256]{0,1:T(8,128)S(1)}, u32[]{:S(2)}, u32[]{:S(2)}) collective-permute-start(f32[512,256]{0,1:T(8,128)S(1)} %fusion.2), channel_id=1, source_target_pairs={{0,1},{1,0},{2,3},{3,2},{4,5},{5,4},{6,7},{7,6},{8,9},{9,8},{10,11... | collective-permute-start | bytes 1572872 | tf_op jit(solution)/shard_map/ppermute | solution.py:46
Sparse Core Ops, SparseCore 0:
  25.2 68.6 all-gather.3

commit v2 on v1

--- a/solution.py
+++ b/solution.py
@@ -18,13 +18,16 @@
     k_half = coupling.shape[1]
     q_half = dist_second.shape[1]
 
-    coupling_x = lax.ppermute(coupling, "zh", [(0, 1), (1, 0)])
-    second_x = lax.ppermute(dist_second, "zh", [(0, 1), (1, 0)])
-
-    piece = jnp.concatenate([coupling, coupling_x], axis=1)
-    into_other_half = [(0, 4), (2, 6), (5, 1), (7, 3)]
-    moved = lax.ppermute(piece, ("yh", "yl", "zh"), into_other_half)
-    piece = jnp.where(yh == zh, piece, moved)
+    message = jnp.concatenate([coupling.reshape(-1), dist_second.reshape(-1)])
+    first = lax.ppermute(message, ("yh", "zh"), [(1, 0), (2, 3), (0, 2), (3, 1)])
+    second = lax.ppermute(message, ("yh", "zh"), [(1, 2), (2, 1)])
+    holds = yh == zh
+    split = coupling.size
+    mine = coupling
+    near = first[:split].reshape(coupling.shape)
+    far = second[:split].reshape(coupling.shape)
+    piece = jnp.where(holds, jnp.concatenate([mine, near], axis=1), jnp.concatenate([near, far], axis=1))
+    second_x = jnp.where(holds, first[split:], second[split:]).reshape(dist_second.shape)
 
     gathered = lax.all_gather(piece, GATHER, axis=0, tiled=True)
 
@@ -51,9 +54,12 @@
     scores = row_potential[:, None] + 2.0 * gradient - column_cost[None, :]
     local_high = jnp.max(scores, axis=0)
     local_sum = jnp.sum(jnp.exp(scores - local_high[None, :]), axis=0)
-    stats = lax.all_gather(jnp.stack([local_high, local_sum]), ROWS, axis=0, tiled=False)
-    highest = jnp.max(stats[:, 0], axis=0)
-    column_sum = jnp.sum(stats[:, 1] * jnp.exp(stats[:, 0] - highest[None, :]), axis=0)
+    pair = jnp.stack([local_high, local_sum])
+    row_count = 64
+    copies = jnp.broadcast_to(pair, (row_count, *pair.shape))
+    pairs = lax.all_to_all(copies, ROWS, 0, 0, tiled=True)
+    highest = jnp.max(pairs[:, 0], axis=0)
+    column_sum = jnp.sum(pairs[:, 1] * jnp.exp(pairs[:, 0] - highest[None, :]), axis=0)
     weights = jnp.exp(scores - highest[None, :])
     potential = jnp.log(column_mass) - highest - jnp.log(column_sum)
     transport = (weights * (N * column_mass / column_sum)[None, :]).astype(jnp.bfloat16)

time: 211 us -> 145 us (0.69)
  blocking collectives: 80.9 us -> 15.7 us
  starting transfers between devices: 15.1 us -> 11.6 us
    all_gather x1 -> x0, blocking collectives: 80.9 us -> none  [body(): lax.all_gather(jnp.stack([local_high, local_sum]), ROWS, axis=0, tiled=Fa...]
    all_to_all x0 -> x1, blocking collectives: none -> 15.7 us  [body(): pairs = lax.all_to_all(copies, ROWS, 0, 0, tiled=True)]
    all_gather x1, waiting for transfers between devices: 63 us -> 67.4 us  [body(): gathered = lax.all_gather(piece, GATHER, axis=0, tiled=True)]
    ppermute x3 -> x2, starting transfers between devices: 12.5 us -> 9.09 us  [the longest x1 8.41 us: body(): lax.ppermute(message, ('yh', 'zh'), [(1, 0), (2, 3), (0, 2), (3, 1)])]
    ppermute x3 -> x2, waiting for transfers between devices: 8.42 us -> 5.03 us  [the longest x1 5.03 us: body(): lax.ppermute(message, ('yh', 'zh'), [(1, 0), (2, 3), (0, 2), (3, 1)])]
  transfers between devices with their start and end apart: 5 -> 4, of which waited for: 5 -> 3; matrix products, arithmetic and copies ran while one was open for 6% -> 9% of each run, Pallas kernels for 0% -> 0%
where the time goes in v2:
time: 145 us
  waiting for transfers between devices  73.1 us (50%)
  matrix products  23.4 us (16%)
  blocking collectives  15.7 us (11%)
  between operations  14.1 us (10%)
  starting transfers between devices  11.6 us (8%)
  other arithmetic  3.98 us (3%)
  local copies, waits for them, and re-layouts  2.91 us (2%)
    all_gather x1, waiting for transfers between devices, body(): gathered = lax.all_gather(piece, GATHER, axis=0, tiled=True)  67.4 us
    dot_general x2, matrix products, partial_gradient(): return jnp.dot(dist_first, product, preferred_element_type=jnp.float32)  23.4 us
    all_to_all x1, blocking collectives, body(): pairs = lax.all_to_all(copies, ROWS, 0, 0, tiled=True)  15.7 us
    ppermute x1, starting transfers between devices, body(): lax.ppermute(message, ('yh', 'zh'), [(1, 0), (2, 3), (0, 2), (3, 1)])  8.41 us
    ppermute x1, waiting for transfers between devices, body(): lax.ppermute(message, ('yh', 'zh'), [(1, 0), (2, 3), (0, 2), (3, 1)])  5.03 us
  transfers between devices with their start and end apart: 4, of which 3 were waited for; matrix products, arithmetic and copies ran while one was open for 9% of the time, Pallas kernels for 0%

profile of v2, /device:TPU:1, one launch (start us, length us, event | category | flops | bytes accessed | tf_op | source)
XLA Modules:
  0.0 144.8 jit_solution(7300152779331123007)
XLA Ops:
  7.2 0.0 all-gather.2.cloned.1.call-start
  7.2 1.0 copy.16
  8.2 0.9 pad_maximum_fusion
  9.1 0.7 collective-permute-start.1
  9.8 8.4 %collective-permute-start = (bf16[131072]{0:T(1024)(128)(2,1)S(1)}, bf16[131072]{0:T(1024)(128)(2,1)S(1)}, u32[]{:S(2)}, u32[]{:S(2)}) collective-permute-start(bf16[131072]{0:T(1024)(128)(2,1)S(1)} %pad_maximum_fusion), channel_id=1, source_target_pairs={{1,0},{64,65},{0,64},{65,1},{3,2},{66,67},{2,66},{67,3},{5,4},{68,... | collective-permute-start | bytes 786440 | tf_op jit(solution)/shard_map/ppermute | solution.py:22
  18.2 0.0 collective-permute-done.1
  18.2 5.0 %collective-permute-done = bf16[131072]{0:T(1024)(128)(2,1)S(1)} collective-permute-done((bf16[131072]{0:T(1024)(128)(2,1)S(1)}, bf16[131072]{0:T(1024)(128)(2,1)S(1)}, u32[]{:S(2)}, u32[]{:S(2)}) %collective-permute-start) | collective-permute-done | bytes 262176 | tf_op jit(solution)/shard_map/ppermute | solution.py:22
  23.3 1.7 %maximum_select_fusion = bf16[512,256]{1,0:T(8,128)(2,1)} fusion(bf16[512,128]{1,0:T(8,128)(2,1)S(1)} %get-tuple-element.17, bf16[512,128]{1,0:T(8,128)(2,1)} %param.7, bf16[512,128]{1,0:T(8,128)(2,1)S(1)} %get-tuple-element.18, pred[]{:T(512)S(6)} %eq.3), kind=kLoop, calls=%fused_computation.10 | loop fusion | flops 1179648 | bytes 655361 | tf_op jit(solution)/shard_map/jit(_where)/select_n | solution.py:29
  25.0 0.0 all-gather.2.cloned.1.call-update
  25.0 0.9 constant_dynamic-update-slice_fusion.1
  26.1 67.4 %all-gather.2.cloned.1.call-done = bf16[16384,256]{1,0:T(8,128)(2,1)} async-done(((bf16[512,256]{1,0:T(8,128)(2,1)}), bf16[16384,256]{1,0:T(8,128)(2,1)}) %all-gather.2.cloned.1.call-update) | async-done | bytes 8388624 | tf_op jit(solution)/shard_map/all_gather | solution.py:32
  93.4 11.7 %fusion.2 = f32[512,256]{0,1:T(8,128)S(1)} fusion(bf16[512,16384]{1,0:T(8,128)(2,1)} %param.6, bf16[16384,256]{1,0:T(8,128)(2,1)} %all-gather.2.cloned.1.call-done, bf16[128,512]{1,0:T(8,128)(2,1)S(1)} %get-tuple-element.14, bf16[128,512]{1,0:T(8,128)(2,1)S(1)} %get-tuple-element.15), kind=kOutput, calls=%fused_computation.4 | convolution fusion | flops 6446907392 | bytes 25952256 | tf_op jit(solution)/shard_map/dot_general | solution.py:46
  105.1 0.0 copy-start
  105.2 0.0 copy-start.1
  105.2 0.0 copy-start.2
  105.2 2.5 %collective-permute-start.2 = (f32[512,256]{0,1:T(8,128)S(1)}, f32[512,256]{0,1:T(8,128)S(1)}, u32[]{:S(2)}, u32[]{:S(2)}) collective-permute-start(f32[512,256]{0,1:T(8,128)S(1)} %fusion.2), channel_id=1, source_target_pairs={{0,1},{1,0},{2,3},{3,2},{4,5},{5,4},{6,7},{7,6},{8,9},{9,8},{10,11... | collective-permute-start | bytes 1572872 | tf_op jit(solution)/shard_map/ppermute | solution.py:49
  107.7 11.7 %fusion.3 = f32[512,256]{0,1:T(8,128)S(1)} fusion(bf16[512,16384]{1,0:T(8,128)(2,1)} %param.6, bf16[16384,256]{1,0:T(8,128)(2,1)} %all-gather.2.cloned.1.call-done, bf16[128,512]{1,0:T(8,128)(2,1)S(1)} %get-tuple-element.15, bf16[128,512]{1,0:T(8,128)(2,1)S(1)} %get-tuple-element.14), kind=kOutput, calls=%fused_computation.5 | convolution fusion | flops 6446907392 | bytes 25952256 | tf_op jit(solution)/shard_map/dot_general | solution.py:46
  119.3 0.7 collective-permute-done.2
  120.0 0.0 copy-done
  120.0 0.0 copy-done.1
  120.0 0.2 fusion.17
  120.2 0.2 exponential_reduce_fusion
  120.5 15.7 %all_to_all.5 = f32[64,2,256]{2,1,0:T(2,128)S(1)} all-to-all(f32[64,2,256]{2,1,0:T(2,128)S(1)} %broadcast_in_dim.2), channel_id=1, replica_groups=mesh['yh'=2,'yl'=2,'x'=4,'zl'=2,'core'=2,'zh'=2] {'yh','yl','x','zl','co..., dimensions={0} | all-to-all | bytes 262144 | tf_op jit(solution)/shard_map/all_to_all | solution.py:60
  136.2 0.1 slice_reduce_fusion
  136.3 0.0 copy-done.2
  136.4 0.6 log_subtract_fusion
  136.9 0.1 multiply_convert_fusion
  137.1 0.8 copy.12
  (7 shorter events, 0.2 us)
Async XLA Ops:
  7.2 86.3 %all-gather.2.cloned.1.call-start = ((), (), s32[]{:S(2)}) async-start(), calls=%async_computation.1 | async-start | bytes 8650752 | tf_op jit(solution)/shard_map/all_gather | solution.py:32
  9.1 9.1 %collective-permute-start.1 = (bf16[131072]{0:T(1024)(128)(2,1)S(1)}, bf16[131072]{0:T(1024)(128)(2,1)S(1)}, u32[]{:S(2)}, u32[]{:S(2)}) collective-permute-start(bf16[131072]{0:T(1024)(128)(2,1)S(1)} %pad_maximum_fusion), channel_id=1, source_target_pairs={{1,64},{64,1},{3,66},{66,3},{5,68},{68,5},{7,70},{70,7},{9,72},{72... | collective-permute-start | bytes 786440 | tf_op jit(solution)/shard_map/ppermute | solution.py:23
  9.8 13.4 %collective-permute-start = (bf16[131072]{0:T(1024)(128)(2,1)S(1)}, bf16[131072]{0:T(1024)(128)(2,1)S(1)}, u32[]{:S(2)}, u32[]{:S(2)}) collective-permute-start(bf16[131072]{0:T(1024)(128)(2,1)S(1)} %pad_maximum_fusion), channel_id=1, source_target_pairs={{1,0},{64,65},{0,64},{65,1},{3,2},{66,67},{2,66},{67,3},{5,4},{68,... | collective-permute-start | bytes 786440 | tf_op jit(solution)/shard_map/ppermute | solution.py:22
  105.1 14.9 %copy-start = (f32[512]{0:T(512)S(1)}, f32[512]{0:T(512)}, u32[]{:S(2)}) copy-start(f32[512]{0:T(512)} %param.9) | copy-start | bytes 6148
  105.2 14.9 %copy-start.1 = (f32[256]{0:T(256)S(1)}, f32[256]{0:T(256)}, u32[]{:S(2)}) copy-start(f32[256]{0:T(256)} %param.10) | copy-start | bytes 3076
  105.2 31.2 %copy-start.2 = (f32[256]{0:T(256)S(1)}, f32[256]{0:T(256)}, u32[]{:S(2)}) copy-start(f32[256]{0:T(256)} %param.11) | copy-start | bytes 3076
  105.2 14.8 %collective-permute-start.2 = (f32[512,256]{0,1:T(8,128)S(1)}, f32[512,256]{0,1:T(8,128)S(1)}, u32[]{:S(2)}, u32[]{:S(2)}) collective-permute-start(f32[512,256]{0,1:T(8,128)S(1)} %fusion.2), channel_id=1, source_target_pairs={{0,1},{1,0},{2,3},{3,2},{4,5},{5,4},{6,7},{7,6},{8,9},{9,8},{10,11... | collective-permute-start | bytes 1572872 | tf_op jit(solution)/shard_map/ppermute | solution.py:49
Sparse Core Ops, SparseCore 0:
  25.1 68.2 all-gather.1

commit v3 on v2

--- a/solution.py
+++ b/solution.py
@@ -18,16 +18,11 @@
     k_half = coupling.shape[1]
     q_half = dist_second.shape[1]
 
-    message = jnp.concatenate([coupling.reshape(-1), dist_second.reshape(-1)])
-    first = lax.ppermute(message, ("yh", "zh"), [(1, 0), (2, 3), (0, 2), (3, 1)])
-    second = lax.ppermute(message, ("yh", "zh"), [(1, 2), (2, 1)])
+    near = lax.ppermute(coupling, ("yh", "zh"), [(1, 0), (2, 3), (0, 2), (3, 1)])
+    far = lax.ppermute(coupling, ("yh", "zh"), [(1, 2), (2, 1)])
     holds = yh == zh
-    split = coupling.size
-    mine = coupling
-    near = first[:split].reshape(coupling.shape)
-    far = second[:split].reshape(coupling.shape)
-    piece = jnp.where(holds, jnp.concatenate([mine, near], axis=1), jnp.concatenate([near, far], axis=1))
-    second_x = jnp.where(holds, first[split:], second[split:]).reshape(dist_second.shape)
+    piece = jnp.where(holds, jnp.concatenate([coupling, near], axis=1), jnp.concatenate([near, far], axis=1))
+    second_x = lax.ppermute(dist_second, "zh", [(0, 1), (1, 0)])
 
     gathered = lax.all_gather(piece, GATHER, axis=0, tiled=True)
 
@@ -39,17 +34,10 @@
         ]
     )
 
-    def partial_gradient(cols):
-        product = jnp.dot(
-            gathered, second_k[:, cols], preferred_element_type=jnp.float32
-        ).astype(jnp.bfloat16)
-        return jnp.dot(dist_first, product, preferred_element_type=jnp.float32)
-
-    other_part = partial_gradient(slice(q_half, 2 * q_half))
-    arrived = lax.ppermute(other_part, "zh", [(0, 1), (1, 0)])
-    own_part = partial_gradient(slice(0, q_half))
-    own_part, arrived = lax.optimization_barrier((own_part, arrived))
-    gradient = own_part + arrived
+    product = jnp.dot(gathered, second_k, preferred_element_type=jnp.float32).astype(jnp.bfloat16)
+    both = jnp.dot(dist_first, product, preferred_element_type=jnp.float32)
+    arrived = lax.ppermute(both[:, q_half:], "zh", [(0, 1), (1, 0)])
+    gradient = both[:, :q_half] + arrived
 
     scores = row_potential[:, None] + 2.0 * gradient - column_cost[None, :]
     local_high = jnp.max(scores, axis=0)

time: 145 us -> 154 us (1.062)
  waiting for transfers between devices: 73.1 us -> 81.5 us
  starting transfers between devices: 11.6 us -> 14.2 us
  local copies, waits for them, and re-layouts: 2.91 us -> 1.07 us
    ppermute x3 -> x4, waiting for transfers between devices: 5.7 us -> 17.4 us  [the longest x1 12.3 us: body(): arrived = lax.ppermute(both[:, q_half:], 'zh', [(0, 1), (1, 0)])]
    all_gather x1, waiting for transfers between devices: 67.4 us -> 64 us  [body(): gathered = lax.all_gather(piece, GATHER, axis=0, tiled=True)]
    ppermute x3 -> x4, starting transfers between devices: 11.6 us -> 14.2 us  [the longest x1 7.25 us: body(): second_x = lax.ppermute(dist_second, 'zh', [(0, 1), (1, 0)])]
    unnamed x9 -> x7, local copies, waits for them, and re-layouts: 2.78 us -> 0.96 us
    dot_general x2 -> x1, matrix products: 23.4 us -> 24.1 us  [body(): both = jnp.dot(dist_first, product, preferred_element_type=jnp.float32)]
  transfers between devices with their start and end apart: 4 -> 5, of which waited for: 3 -> 4; matrix products, arithmetic and copies ran while one was open for 9% -> 1% of each run, Pallas kernels for 0% -> 0%
where the time goes in v3:
time: 154 us
  waiting for transfers between devices  81.5 us (53%)
  matrix products  24.1 us (16%)
  blocking collectives  15.7 us (10%)
  starting transfers between devices  14.2 us (9%)
  between operations  14.1 us (9%)
  other arithmetic  3.55 us (2%)
    all_gather x1, waiting for transfers between devices, body(): gathered = lax.all_gather(piece, GATHER, axis=0, tiled=True)  64 us
    dot_general x1, matrix products, body(): both = jnp.dot(dist_first, product, preferred_element_type=jnp.float32)  24.1 us
    all_to_all x1, blocking collectives, body(): pairs = lax.all_to_all(copies, ROWS, 0, 0, tiled=True)  15.7 us
    ppermute x1, waiting for transfers between devices, body(): arrived = lax.ppermute(both[:, q_half:], 'zh', [(0, 1), (1, 0)])  12.3 us
    ppermute x1, starting transfers between devices, body(): second_x = lax.ppermute(dist_second, 'zh', [(0, 1), (1, 0)])  7.25 us
    ppermute x1, starting transfers between devices, body(): lax.ppermute(coupling, ('yh', 'zh'), [(1, 0), (2, 3), (0, 2), (3, 1)])  3.81 us
    ppermute x1, waiting for transfers between devices, body(): lax.ppermute(coupling, ('yh', 'zh'), [(1, 0), (2, 3), (0, 2), (3, 1)])  3.44 us
  transfers between devices with their start and end apart: 5, of which 4 were waited for; matrix products, arithmetic and copies ran while one was open for 1% of the time, Pallas kernels for 0%

profile of v3, /device:TPU:1, one launch (start us, length us, event | category | flops | bytes accessed | tf_op | source)
XLA Modules:
  0.0 154.2 jit_solution(3849723674158851873)
XLA Ops:
  7.2 0.0 all-gather.2.cloned.1.call-start
  7.2 3.8 %collective-permute-start = (bf16[512,128]{1,0:T(8,128)(2,1)}, bf16[512,128]{1,0:T(8,128)(2,1)S(1)}, u32[]{:S(2)}, u32[]{:S(2)}) collective-permute-start(bf16[512,128]{1,0:T(8,128)(2,1)} %param.7), channel_id=1, source_target_pairs={{1,0},{64,65},{0,64},{65,1},{3,2},{66,67},{2,66},{67,3},{5,4},{68,... | collective-permute-start | bytes 393224 | tf_op jit(solution)/shard_map/ppermute | solution.py:21
  11.0 0.7 collective-permute-start.1
  11.7 3.4 %collective-permute-done = bf16[512,128]{1,0:T(8,128)(2,1)S(1)} collective-permute-done((bf16[512,128]{1,0:T(8,128)(2,1)}, bf16[512,128]{1,0:T(8,128)(2,1)S(1)}, u32[]{:S(2)}, u32[]{:S(2)}) %collective-permute-start) | collective-permute-done | bytes 131104 | tf_op jit(solution)/shard_map/ppermute | solution.py:21
  15.1 0.0 collective-permute-done.1
  15.1 1.7 %maximum_select_fusion = bf16[512,256]{1,0:T(8,128)(2,1)} fusion(bf16[512,128]{1,0:T(8,128)(2,1)S(1)} %collective-permute-done, bf16[512,128]{1,0:T(8,128)(2,1)} %param.7, bf16[512,128]{1,0:T(8,128)(2,1)S(1)} %collective-permute-done.1, pred[]{:T(512)S(6)} %eq.3), kind=kLoop, calls=%fused_computation.9 | loop fusion | flops 1179648 | bytes 655361 | tf_op jit(solution)/shard_map/jit(_where)/select_n | solution.py:24
  16.8 0.0 all-gather.2.cloned.1.call-update
  16.8 7.2 %collective-permute-start.2 = (bf16[256,256]{1,0:T(8,128)(2,1)}, bf16[256,256]{1,0:T(8,128)(2,1)S(1)}, u32[]{:S(2)}, u32[]{:S(2)}) collective-permute-start(bf16[256,256]{1,0:T(8,128)(2,1)} %param.8), channel_id=1, source_target_pairs={{0,1},{1,0},{2,3},{3,2},{4,5},{5,4},{6,7},{7,6},{8,9},{9,8},{10,11... | collective-permute-start | bytes 393224 | tf_op jit(solution)/shard_map/ppermute | solution.py:25
  24.1 0.9 constant_dynamic-update-slice_fusion.1
  25.0 1.6 %collective-permute-done.2 = bf16[256,256]{1,0:T(8,128)(2,1)S(1)} collective-permute-done((bf16[256,256]{1,0:T(8,128)(2,1)}, bf16[256,256]{1,0:T(8,128)(2,1)S(1)}, u32[]{:S(2)}, u32[]{:S(2)}) %collective-permute-start.2) | collective-permute-done | bytes 131104 | tf_op jit(solution)/shard_map/ppermute | solution.py:25
  26.7 64.0 %all-gather.2.cloned.1.call-done = bf16[16384,256]{1,0:T(8,128)(2,1)} async-done(((bf16[512,256]{1,0:T(8,128)(2,1)}), bf16[16384,256]{1,0:T(8,128)(2,1)}) %all-gather.2.cloned.1.call-update) | async-done | bytes 8388624 | tf_op jit(solution)/shard_map/all_gather | solution.py:27
  90.8 0.0 copy-start
  90.8 0.0 copy-start.1
  90.8 0.0 copy-start.2
  90.8 24.1 %fusion.1 = f32[512,512]{1,0:T(8,128)S(1)} fusion(bf16[512,16384]{1,0:T(8,128)(2,1)} %param.6, bf16[16384,256]{1,0:T(8,128)(2,1)} %all-gather.2.cloned.1.call-done, bf16[128,512]{1,0:T(8,128)(2,1)S(1)} %get-tuple-element.5, bf16[128,512]{1,0:T(8,128)(2,1)S(1)} %get-tuple-element.4), kind=kOutput, calls=%fused_computation.2 | convolution fusion | flops 12893814784 | bytes 26476544 | tf_op jit(solution)/shard_map/dot_general | solution.py:38
  114.9 2.5 %collective-permute-start.3 = (f32[512,256]{1,0:T(8,128)S(1)}, f32[512,256]{1,0:T(8,128)S(1)}, u32[]{:S(2)}, u32[]{:S(2)}) collective-permute-start(f32[512,256]{1,0:T(8,128)S(1)} %slice.18), channel_id=1, source_target_pairs={{0,1},{1,0},{2,3},{3,2},{4,5},{5,4},{6,7},{7,6},{8,9},{9,8},{10,11... | collective-permute-start | bytes 1572872 | tf_op jit(solution)/shard_map/ppermute | solution.py:39
  117.4 12.3 %collective-permute-done.3 = f32[512,256]{1,0:T(8,128)S(1)} collective-permute-done((f32[512,256]{1,0:T(8,128)S(1)}, f32[512,256]{1,0:T(8,128)S(1)}, u32[]{:S(2)}, u32[]{:S(2)}) %collective-permute-start.3) | collective-permute-done | bytes 524320 | tf_op jit(solution)/shard_map/ppermute | solution.py:39
  129.7 0.0 copy-done
  129.7 0.0 copy-done.1
  129.7 0.2 fusion.17
  129.9 0.1 exponential_reduce_fusion
  130.1 15.7 %all_to_all.5 = f32[64,2,256]{2,1,0:T(2,128)S(1)} all-to-all(f32[64,2,256]{2,1,0:T(2,128)S(1)} %broadcast_in_dim.2), channel_id=1, replica_groups=mesh['yh'=2,'yl'=2,'x'=4,'zl'=2,'core'=2,'zh'=2] {'yh','yl','x','zl','co..., dimensions={0} | all-to-all | bytes 262144 | tf_op jit(solution)/shard_map/all_to_all | solution.py:48
  145.8 0.1 slice_reduce_fusion
  146.0 0.0 copy-done.2
  146.0 0.6 log_subtract_fusion
  146.5 0.8 multiply_convert_fusion
  (6 shorter events, 0.2 us)
Async XLA Ops:
  7.2 83.6 %all-gather.2.cloned.1.call-start = ((), (), s32[]{:S(2)}) async-start(), calls=%async_computation.1 | async-start | bytes 8650752 | tf_op jit(solution)/shard_map/all_gather | solution.py:27
  7.2 7.9 %collective-permute-start = (bf16[512,128]{1,0:T(8,128)(2,1)}, bf16[512,128]{1,0:T(8,128)(2,1)S(1)}, u32[]{:S(2)}, u32[]{:S(2)}) collective-permute-start(bf16[512,128]{1,0:T(8,128)(2,1)} %param.7), channel_id=1, source_target_pairs={{1,0},{64,65},{0,64},{65,1},{3,2},{66,67},{2,66},{67,3},{5,4},{68,... | collective-permute-start | bytes 393224 | tf_op jit(solution)/shard_map/ppermute | solution.py:21
  11.0 4.1 %collective-permute-start.1 = (bf16[512,128]{1,0:T(8,128)(2,1)}, bf16[512,128]{1,0:T(8,128)(2,1)S(1)}, u32[]{:S(2)}, u32[]{:S(2)}) collective-permute-start(bf16[512,128]{1,0:T(8,128)(2,1)} %param.7), channel_id=1, source_target_pairs={{1,64},{64,1},{3,66},{66,3},{5,68},{68,5},{7,70},{70,7},{9,72},{72... | collective-permute-start | bytes 393224 | tf_op jit(solution)/shard_map/ppermute | solution.py:22
  16.8 9.8 %collective-permute-start.2 = (bf16[256,256]{1,0:T(8,128)(2,1)}, bf16[256,256]{1,0:T(8,128)(2,1)S(1)}, u32[]{:S(2)}, u32[]{:S(2)}) collective-permute-start(bf16[256,256]{1,0:T(8,128)(2,1)} %param.8), channel_id=1, source_target_pairs={{0,1},{1,0},{2,3},{3,2},{4,5},{5,4},{6,7},{7,6},{8,9},{9,8},{10,11... | collective-permute-start | bytes 393224 | tf_op jit(solution)/shard_map/ppermute | solution.py:25
  90.8 39.0 %copy-start = (f32[512]{0:T(512)S(1)}, f32[512]{0:T(512)}, u32[]{:S(2)}) copy-start(f32[512]{0:T(512)} %param.9) | copy-start | bytes 6148
  90.8 39.0 %copy-start.1 = (f32[256]{0:T(256)S(1)}, f32[256]{0:T(256)}, u32[]{:S(2)}) copy-start(f32[256]{0:T(256)} %param.10) | copy-start | bytes 3076
  90.8 55.2 %copy-start.2 = (f32[256]{0:T(256)S(1)}, f32[256]{0:T(256)}, u32[]{:S(2)}) copy-start(f32[256]{0:T(256)} %param.11) | copy-start | bytes 3076
  114.9 14.8 %collective-permute-start.3 = (f32[512,256]{1,0:T(8,128)S(1)}, f32[512,256]{1,0:T(8,128)S(1)}, u32[]{:S(2)}, u32[]{:S(2)}) collective-permute-start(f32[512,256]{1,0:T(8,128)S(1)} %slice.18), channel_id=1, source_target_pairs={{0,1},{1,0},{2,3},{3,2},{4,5},{5,4},{6,7},{7,6},{8,9},{9,8},{10,11... | collective-permute-start | bytes 1572872 | tf_op jit(solution)/shard_map/ppermute | solution.py:39
Sparse Core Ops, SparseCore 0:
  17.0 73.7 all-gather.1

commit v4 on v2

--- a/solution.py
+++ b/solution.py
@@ -18,16 +18,11 @@
     k_half = coupling.shape[1]
     q_half = dist_second.shape[1]
 
-    message = jnp.concatenate([coupling.reshape(-1), dist_second.reshape(-1)])
-    first = lax.ppermute(message, ("yh", "zh"), [(1, 0), (2, 3), (0, 2), (3, 1)])
-    second = lax.ppermute(message, ("yh", "zh"), [(1, 2), (2, 1)])
+    near = lax.ppermute(coupling, ("yh", "zh"), [(1, 0), (2, 3), (0, 2), (3, 1)])
+    far = lax.ppermute(coupling, ("yh", "zh"), [(1, 2), (2, 1)])
     holds = yh == zh
-    split = coupling.size
-    mine = coupling
-    near = first[:split].reshape(coupling.shape)
-    far = second[:split].reshape(coupling.shape)
-    piece = jnp.where(holds, jnp.concatenate([mine, near], axis=1), jnp.concatenate([near, far], axis=1))
-    second_x = jnp.where(holds, first[split:], second[split:]).reshape(dist_second.shape)
+    piece = jnp.where(holds, jnp.concatenate([coupling, near], axis=1), jnp.concatenate([near, far], axis=1))
+    second_x = lax.ppermute(dist_second, "zh", [(0, 1), (1, 0)])
 
     gathered = lax.all_gather(piece, GATHER, axis=0, tiled=True)
 

time: 145 us -> 142 us (0.979)
  waiting for transfers between devices: 73.1 us -> 69.8 us
  starting transfers between devices: 11.6 us -> 14.2 us
    all_gather x1, waiting for transfers between devices: 67.4 us -> 64 us  [body(): gathered = lax.all_gather(piece, GATHER, axis=0, tiled=True)]
    ppermute x2 -> x3, starting transfers between devices: 9.09 us -> 11.7 us  [the longest x1 7.25 us: body(): second_x = lax.ppermute(dist_second, 'zh', [(0, 1), (1, 0)])]
    ppermute x2 -> x3, waiting for transfers between devices: 5.03 us -> 5.07 us  [the longest x1 3.44 us: body(): lax.ppermute(coupling, ('yh', 'zh'), [(1, 0), (2, 3), (0, 2), (3, 1)])]
  transfers between devices with their start and end apart: 4 -> 5, of which waited for: 3 -> 4; matrix products, arithmetic and copies ran while one was open for 9% -> 9% of each run, Pallas kernels for 0% -> 0%
where the time goes in v4:
time: 142 us
  waiting for transfers between devices  69.8 us (49%)
  matrix products  23.4 us (16%)
  blocking collectives  15.7 us (11%)
  starting transfers between devices  14.2 us (10%)
  between operations  14.1 us (10%)
  other arithmetic  3.02 us (2%)
  local copies, waits for them, and re-layouts  1.88 us (1%)
    all_gather x1, waiting for transfers between devices, body(): gathered = lax.all_gather(piece, GATHER, axis=0, tiled=True)  64 us
    dot_general x2, matrix products, partial_gradient(): return jnp.dot(dist_first, product, preferred_element_type=jnp.float32)  23.4 us
    all_to_all x1, blocking collectives, body(): pairs = lax.all_to_all(copies, ROWS, 0, 0, tiled=True)  15.7 us
    ppermute x1, starting transfers between devices, body(): second_x = lax.ppermute(dist_second, 'zh', [(0, 1), (1, 0)])  7.25 us
    ppermute x1, starting transfers between devices, body(): lax.ppermute(coupling, ('yh', 'zh'), [(1, 0), (2, 3), (0, 2), (3, 1)])  3.81 us
    ppermute x1, waiting for transfers between devices, body(): lax.ppermute(coupling, ('yh', 'zh'), [(1, 0), (2, 3), (0, 2), (3, 1)])  3.44 us
  transfers between devices with their start and end apart: 5, of which 4 were waited for; matrix products, arithmetic and copies ran while one was open for 9% of the time, Pallas kernels for 0%

profile of v4, /device:TPU:1, one launch (start us, length us, event | category | flops | bytes accessed | tf_op | source)
XLA Modules:
  0.0 142.1 jit_solution(16908365504601601446)
XLA Ops:
  7.2 0.0 all-gather.2.cloned.1.call-start
  7.2 3.8 %collective-permute-start = (bf16[512,128]{1,0:T(8,128)(2,1)}, bf16[512,128]{1,0:T(8,128)(2,1)S(1)}, u32[]{:S(2)}, u32[]{:S(2)}) collective-permute-start(bf16[512,128]{1,0:T(8,128)(2,1)} %param.7), channel_id=1, source_target_pairs={{1,0},{64,65},{0,64},{65,1},{3,2},{66,67},{2,66},{67,3},{5,4},{68,... | collective-permute-start | bytes 393224 | tf_op jit(solution)/shard_map/ppermute | solution.py:21
  11.0 0.7 collective-permute-start.1
  11.7 3.4 %collective-permute-done = bf16[512,128]{1,0:T(8,128)(2,1)S(1)} collective-permute-done((bf16[512,128]{1,0:T(8,128)(2,1)}, bf16[512,128]{1,0:T(8,128)(2,1)S(1)}, u32[]{:S(2)}, u32[]{:S(2)}) %collective-permute-start) | collective-permute-done | bytes 131104 | tf_op jit(solution)/shard_map/ppermute | solution.py:21
  15.1 0.0 collective-permute-done.1
  15.1 1.7 %maximum_select_fusion = bf16[512,256]{1,0:T(8,128)(2,1)} fusion(bf16[512,128]{1,0:T(8,128)(2,1)S(1)} %collective-permute-done, bf16[512,128]{1,0:T(8,128)(2,1)} %param.7, bf16[512,128]{1,0:T(8,128)(2,1)S(1)} %collective-permute-done.1, pred[]{:T(512)S(6)} %eq.3), kind=kLoop, calls=%fused_computation.9 | loop fusion | flops 1179648 | bytes 655361 | tf_op jit(solution)/shard_map/jit(_where)/select_n | solution.py:24
  16.8 0.0 all-gather.2.cloned.1.call-update
  16.8 7.2 %collective-permute-start.2 = (bf16[256,256]{1,0:T(8,128)(2,1)}, bf16[256,256]{1,0:T(8,128)(2,1)S(1)}, u32[]{:S(2)}, u32[]{:S(2)}) collective-permute-start(bf16[256,256]{1,0:T(8,128)(2,1)} %param.8), channel_id=1, source_target_pairs={{0,1},{1,0},{2,3},{3,2},{4,5},{5,4},{6,7},{7,6},{8,9},{9,8},{10,11... | collective-permute-start | bytes 393224 | tf_op jit(solution)/shard_map/ppermute | solution.py:25
  24.1 0.9 constant_dynamic-update-slice_fusion.1
  25.0 1.6 %collective-permute-done.2 = bf16[256,256]{1,0:T(8,128)(2,1)S(1)} collective-permute-done((bf16[256,256]{1,0:T(8,128)(2,1)}, bf16[256,256]{1,0:T(8,128)(2,1)S(1)}, u32[]{:S(2)}, u32[]{:S(2)}) %collective-permute-start.2) | collective-permute-done | bytes 131104 | tf_op jit(solution)/shard_map/ppermute | solution.py:25
  26.7 64.0 %all-gather.2.cloned.1.call-done = bf16[16384,256]{1,0:T(8,128)(2,1)} async-done(((bf16[512,256]{1,0:T(8,128)(2,1)}), bf16[16384,256]{1,0:T(8,128)(2,1)}) %all-gather.2.cloned.1.call-update) | async-done | bytes 8388624 | tf_op jit(solution)/shard_map/all_gather | solution.py:27
  90.8 11.7 %fusion.2 = f32[512,256]{0,1:T(8,128)S(1)} fusion(bf16[512,16384]{1,0:T(8,128)(2,1)} %param.6, bf16[16384,256]{1,0:T(8,128)(2,1)} %all-gather.2.cloned.1.call-done, bf16[128,512]{1,0:T(8,128)(2,1)S(1)} %get-tuple-element.14, bf16[128,512]{1,0:T(8,128)(2,1)S(1)} %get-tuple-element.15), kind=kOutput, calls=%fused_computation.4 | convolution fusion | flops 6446907392 | bytes 25952256 | tf_op jit(solution)/shard_map/dot_general | solution.py:41
  102.5 0.0 copy-start
  102.5 0.0 copy-start.1
  102.5 0.0 copy-start.2
  102.5 2.5 %collective-permute-start.3 = (f32[512,256]{0,1:T(8,128)S(1)}, f32[512,256]{0,1:T(8,128)S(1)}, u32[]{:S(2)}, u32[]{:S(2)}) collective-permute-start(f32[512,256]{0,1:T(8,128)S(1)} %fusion.2), channel_id=1, source_target_pairs={{0,1},{1,0},{2,3},{3,2},{4,5},{5,4},{6,7},{7,6},{8,9},{9,8},{10,11... | collective-permute-start | bytes 1572872 | tf_op jit(solution)/shard_map/ppermute | solution.py:44
  105.0 11.7 %fusion.3 = f32[512,256]{0,1:T(8,128)S(1)} fusion(bf16[512,16384]{1,0:T(8,128)(2,1)} %param.6, bf16[16384,256]{1,0:T(8,128)(2,1)} %all-gather.2.cloned.1.call-done, bf16[128,512]{1,0:T(8,128)(2,1)S(1)} %get-tuple-element.15, bf16[128,512]{1,0:T(8,128)(2,1)S(1)} %get-tuple-element.14), kind=kOutput, calls=%fused_computation.5 | convolution fusion | flops 6446907392 | bytes 25952256 | tf_op jit(solution)/shard_map/dot_general | solution.py:41
  116.7 0.7 collective-permute-done.3
  117.3 0.0 copy-done
  117.3 0.0 copy-done.1
  117.3 0.2 fusion.17
  117.5 0.2 exponential_reduce_fusion
  117.8 15.7 %all_to_all.5 = f32[64,2,256]{2,1,0:T(2,128)S(1)} all-to-all(f32[64,2,256]{2,1,0:T(2,128)S(1)} %broadcast_in_dim.2), channel_id=1, replica_groups=mesh['yh'=2,'yl'=2,'x'=4,'zl'=2,'core'=2,'zh'=2] {'yh','yl','x','zl','co..., dimensions={0} | all-to-all | bytes 262144 | tf_op jit(solution)/shard_map/all_to_all | solution.py:55
  133.5 0.1 slice_reduce_fusion
  133.7 0.0 copy-done.2
  133.7 0.6 log_subtract_fusion
  134.2 0.1 multiply_convert_fusion
  134.4 0.8 copy.12
  (5 shorter events, 0.1 us)
Async XLA Ops:
  7.2 83.6 %all-gather.2.cloned.1.call-start = ((), (), s32[]{:S(2)}) async-start(), calls=%async_computation.1 | async-start | bytes 8650752 | tf_op jit(solution)/shard_map/all_gather | solution.py:27
  7.2 7.9 %collective-permute-start = (bf16[512,128]{1,0:T(8,128)(2,1)}, bf16[512,128]{1,0:T(8,128)(2,1)S(1)}, u32[]{:S(2)}, u32[]{:S(2)}) collective-permute-start(bf16[512,128]{1,0:T(8,128)(2,1)} %param.7), channel_id=1, source_target_pairs={{1,0},{64,65},{0,64},{65,1},{3,2},{66,67},{2,66},{67,3},{5,4},{68,... | collective-permute-start | bytes 393224 | tf_op jit(solution)/shard_map/ppermute | solution.py:21
  11.0 4.1 %collective-permute-start.1 = (bf16[512,128]{1,0:T(8,128)(2,1)}, bf16[512,128]{1,0:T(8,128)(2,1)S(1)}, u32[]{:S(2)}, u32[]{:S(2)}) collective-permute-start(bf16[512,128]{1,0:T(8,128)(2,1)} %param.7), channel_id=1, source_target_pairs={{1,64},{64,1},{3,66},{66,3},{5,68},{68,5},{7,70},{70,7},{9,72},{72... | collective-permute-start | bytes 393224 | tf_op jit(solution)/shard_map/ppermute | solution.py:22
  16.8 9.8 %collective-permute-start.2 = (bf16[256,256]{1,0:T(8,128)(2,1)}, bf16[256,256]{1,0:T(8,128)(2,1)S(1)}, u32[]{:S(2)}, u32[]{:S(2)}) collective-permute-start(bf16[256,256]{1,0:T(8,128)(2,1)} %param.8), channel_id=1, source_target_pairs={{0,1},{1,0},{2,3},{3,2},{4,5},{5,4},{6,7},{7,6},{8,9},{9,8},{10,11... | collective-permute-start | bytes 393224 | tf_op jit(solution)/shard_map/ppermute | solution.py:25
  102.5 14.9 %copy-start = (f32[512]{0:T(512)S(1)}, f32[512]{0:T(512)}, u32[]{:S(2)}) copy-start(f32[512]{0:T(512)} %param.9) | copy-start | bytes 6148
  102.5 14.9 %copy-start.1 = (f32[256]{0:T(256)S(1)}, f32[256]{0:T(256)}, u32[]{:S(2)}) copy-start(f32[256]{0:T(256)} %param.10) | copy-start | bytes 3076
  102.5 31.2 %copy-start.2 = (f32[256]{0:T(256)S(1)}, f32[256]{0:T(256)}, u32[]{:S(2)}) copy-start(f32[256]{0:T(256)} %param.11) | copy-start | bytes 3076
  102.5 14.8 %collective-permute-start.3 = (f32[512,256]{0,1:T(8,128)S(1)}, f32[512,256]{0,1:T(8,128)S(1)}, u32[]{:S(2)}, u32[]{:S(2)}) collective-permute-start(f32[512,256]{0,1:T(8,128)S(1)} %fusion.2), channel_id=1, source_target_pairs={{0,1},{1,0},{2,3},{3,2},{4,5},{5,4},{6,7},{7,6},{8,9},{9,8},{10,11... | collective-permute-start | bytes 1572872 | tf_op jit(solution)/shard_map/ppermute | solution.py:44
Sparse Core Ops, SparseCore 0:
  17.0 73.7 all-gather.1

commit v5 on v4

--- a/solution.py
+++ b/solution.py
@@ -2,6 +2,8 @@
 import jax.numpy as jnp
 import numpy as np
 from jax import lax
+from jax.experimental import pallas as pl
+from jax.experimental.pallas import tpu as pltpu
 from jax.sharding import Mesh
 from jax.sharding import PartitionSpec as P
 
@@ -9,6 +11,34 @@
 AXES = ("yh", "yl", "x", "zl", "core", "zh")
 ROWS = ("yh", "yl", "x", "zl", "core")
 GATHER = ("yl", "x", "zl", "core")
+
+
+def _panel_kernel(d_ref, c_ref, s_ref, o_ref):
+    @pl.when(pl.program_id(0) == 0)
+    def _():
+        o_ref[...] = jnp.zeros_like(o_ref)
+    product = jnp.dot(c_ref[...], s_ref[...], preferred_element_type=jnp.float32).astype(jnp.bfloat16)
+    o_ref[...] += jnp.dot(d_ref[...], product, preferred_element_type=jnp.float32)
+
+def panel_gradient(dist_first, coupling_rows, second_cols, step=2048):
+    rows, inner = dist_first.shape
+    k = coupling_rows.shape[1]
+    q = second_cols.shape[1]
+    flops = 2 * inner * k * q + 2 * rows * inner * q
+    bytes_accessed = 2 * (dist_first.size + coupling_rows.size + second_cols.size) + 4 * rows * q
+    return pl.pallas_call(
+        _panel_kernel,
+        out_shape=jax.ShapeDtypeStruct((rows, q), jnp.float32),
+        grid=(inner // step,),
+        in_specs=[
+            pl.BlockSpec((rows, step), lambda j: (0, j)),
+            pl.BlockSpec((step, k), lambda j: (j, 0)),
+            pl.BlockSpec((k, q), lambda j: (0, 0)),
+        ],
+        out_specs=pl.BlockSpec((rows, q), lambda j: (0, 0)),
+        compiler_params=pltpu.CompilerParams(dimension_semantics=("arbitrary",)),
+        cost_estimate=pl.CostEstimate(flops=flops, transcendentals=0, bytes_accessed=bytes_accessed),
+    )(dist_first, coupling_rows, second_cols)
 
 
 def body(dist_first, coupling, dist_second, row_potential, column_cost, column_mass):
@@ -35,10 +65,7 @@
     )
 
     def partial_gradient(cols):
-        product = jnp.dot(
-            gathered, second_k[:, cols], preferred_element_type=jnp.float32
-        ).astype(jnp.bfloat16)
-        return jnp.dot(dist_first, product, preferred_element_type=jnp.float32)
+        return panel_gradient(dist_first, gathered, second_k[:, cols])
 
     other_part = partial_gradient(slice(q_half, 2 * q_half))
     arrived = lax.ppermute(other_part, "zh", [(0, 1), (1, 0)])

time: 142 us -> 150 us (1.056)
  Pallas kernels: 0 us -> 31.5 us
  matrix products: 23.4 us -> 0 us
  other arithmetic: 3.02 us -> 5.28 us
    pallas_call x0 -> x2, Pallas kernels: none -> 31.5 us  [panel_gradient(): pl.pallas_call(_panel_kernel, out_shape=jax.ShapeDtypeStruct((rows, q), j...]
    dot_general x2 -> x0, matrix products: 23.4 us -> none  [partial_gradient(): return jnp.dot(dist_first, product, preferred_element_type=jnp.float32)]
  transfers between devices with their start and end apart: 5 -> 5, of which waited for: 4 -> 3; matrix products, arithmetic and copies ran while one was open for 9% -> 1% of each run, Pallas kernels for 0% -> 11%
where the time goes in v5:
time: 150 us; the launch traced here: 149 us
  waiting for transfers between devices  68.4 us (46%)
  Pallas kernels  31.5 us (21%)
  blocking collectives  14.8 us (10%)
  starting transfers between devices  14.2 us (9%)
  between operations  14.1 us (9%)
  other arithmetic  5.28 us (4%)
    all_gather x1, waiting for transfers between devices, body(): gathered = lax.all_gather(piece, GATHER, axis=0, tiled=True)  63.3 us
    pallas_call x2, Pallas kernels, panel_gradient(): pl.pallas_call(_panel_kernel, out_shape=jax.ShapeDtypeStruct((rows, q), j...  31.5 us
    all_to_all x1, blocking collectives, body(): pairs = lax.all_to_all(copies, ROWS, 0, 0, tiled=True)  14.8 us
    ppermute x1, starting transfers between devices, body(): second_x = lax.ppermute(dist_second, 'zh', [(0, 1), (1, 0)])  7.25 us
    ppermute x1, starting transfers between devices, body(): lax.ppermute(coupling, ('yh', 'zh'), [(1, 0), (2, 3), (0, 2), (3, 1)])  3.81 us
    ppermute x1, waiting for transfers between devices, body(): lax.ppermute(coupling, ('yh', 'zh'), [(1, 0), (2, 3), (0, 2), (3, 1)])  3.44 us
  transfers between devices with their start and end apart: 5, of which 3 were waited for; matrix products, arithmetic and copies ran while one was open for 1% of the time, Pallas kernels for 11%

profile of v5, /device:TPU:1, one launch (start us, length us, event | category | flops | bytes accessed | tf_op | source)
XLA Modules:
  0.0 149.3 jit_solution(7481976214295154977)
XLA Ops:
  7.2 0.0 all-gather.2.cloned.1.call-start
  7.2 3.8 %collective-permute-start = (bf16[512,128]{1,0:T(8,128)(2,1)}, bf16[512,128]{1,0:T(8,128)(2,1)S(1)}, u32[]{:S(2)}, u32[]{:S(2)}) collective-permute-start(bf16[512,128]{1,0:T(8,128)(2,1)} %param.7), channel_id=1, source_target_pairs={{1,0},{64,65},{0,64},{65,1},{3,2},{66,67},{2,66},{67,3},{5,4},{68,... | collective-permute-start | bytes 393224 | tf_op jit(solution)/shard_map/ppermute | solution.py:51
  11.0 0.7 collective-permute-start.1
  11.7 3.4 %collective-permute-done = bf16[512,128]{1,0:T(8,128)(2,1)S(1)} collective-permute-done((bf16[512,128]{1,0:T(8,128)(2,1)}, bf16[512,128]{1,0:T(8,128)(2,1)S(1)}, u32[]{:S(2)}, u32[]{:S(2)}) %collective-permute-start) | collective-permute-done | bytes 131104 | tf_op jit(solution)/shard_map/ppermute | solution.py:51
  15.1 0.0 collective-permute-done.1
  15.1 1.7 %maximum_select_fusion = bf16[512,256]{1,0:T(8,128)(2,1)} fusion(bf16[512,128]{1,0:T(8,128)(2,1)S(1)} %collective-permute-done, bf16[512,128]{1,0:T(8,128)(2,1)} %param.7, bf16[512,128]{1,0:T(8,128)(2,1)S(1)} %collective-permute-done.1, pred[]{:T(512)S(6)} %eq.3), kind=kLoop, calls=%fused_computation.3 | loop fusion | flops 1179648 | bytes 655361 | tf_op jit(solution)/shard_map/jit(_where)/select_n | solution.py:54
  16.8 0.0 all-gather.2.cloned.1.call-update
  16.8 7.2 %collective-permute-start.2 = (bf16[256,256]{1,0:T(8,128)(2,1)}, bf16[256,256]{1,0:T(8,128)(2,1)S(1)}, u32[]{:S(2)}, u32[]{:S(2)}) collective-permute-start(bf16[256,256]{1,0:T(8,128)(2,1)} %param.8), channel_id=1, source_target_pairs={{0,1},{1,0},{2,3},{3,2},{4,5},{5,4},{6,7},{7,6},{8,9},{9,8},{10,11... | collective-permute-start | bytes 393224 | tf_op jit(solution)/shard_map/ppermute | solution.py:55
  24.1 0.9 constant_dynamic-update-slice_fusion.1
  25.0 1.6 %collective-permute-done.2 = bf16[256,256]{1,0:T(8,128)(2,1)S(1)} collective-permute-done((bf16[256,256]{1,0:T(8,128)(2,1)}, bf16[256,256]{1,0:T(8,128)(2,1)S(1)}, u32[]{:S(2)}, u32[]{:S(2)}) %collective-permute-start.2) | collective-permute-done | bytes 131104 | tf_op jit(solution)/shard_map/ppermute | solution.py:55
  26.7 0.7 pad_maximum_fusion
  27.4 63.3 %all-gather.2.cloned.1.call-done.c_ref = bf16[16384,256]{1,0:T(8,128)(2,1)} async-done(((bf16[512,256]{1,0:T(8,128)(2,1)}), bf16[16384,256]{1,0:T(8,128)(2,1)}) %all-gather.2.cloned.1.call-update) | async-done | bytes 8388624 | tf_op jit(solution)/shard_map/all_gather | solution.py:57
  90.8 15.8 %shard_map.78 = f32[512,256]{1,0:T(8,128)} custom-call(bf16[512,16384]{1,0:T(8,128)(2,1)} %d_ref.3, bf16[16384,256]{1,0:T(8,128)(2,1)} %all-gather.2.cloned.1.call-done.c_ref, bf16[256,256]{1,0:T(8,128)(2,1)} %get-tuple-element.8.s_ref), custom_call_target="tpu_custom_call" | custom-call | flops 6442450944 | bytes 25821184 | tf_op jit(solution)/shard_map/pallas_call | solution.py:29
  106.5 0.0 copy-start
  106.5 0.0 copy-start.1
  106.5 0.0 copy-start.2
  106.5 2.5 %collective-permute-start.3 = (f32[512,256]{1,0:T(8,128)}, f32[512,256]{1,0:T(8,128)S(1)}, u32[]{:S(2)}, u32[]{:S(2)}) collective-permute-start(f32[512,256]{1,0:T(8,128)} %shard_map.78), channel_id=1, source_target_pairs={{0,1},{1,0},{2,3},{3,2},{4,5},{5,4},{6,7},{7,6},{8,9},{9,8},{10,11... | collective-permute-start | bytes 1572872 | tf_op jit(solution)/shard_map/ppermute | solution.py:71
  109.0 15.8 %shard_map.77 = f32[512,256]{1,0:T(8,128)} custom-call(bf16[512,16384]{1,0:T(8,128)(2,1)} %d_ref.3, bf16[16384,256]{1,0:T(8,128)(2,1)} %all-gather.2.cloned.1.call-done.c_ref, bf16[256,256]{1,0:T(8,128)(2,1)} %get-tuple-element.9.s_ref), custom_call_target="tpu_custom_call" | custom-call | flops 6442450944 | bytes 25821184 | tf_op jit(solution)/shard_map/pallas_call | solution.py:29
  124.8 0.0 collective-permute-done.3
  124.8 0.0 copy-done
  124.8 0.0 copy-done.1
  124.8 1.2 fusion.5
  126.0 0.1 exponential_reduce_fusion
  126.2 14.8 %all_to_all.5 = f32[64,2,256]{2,1,0:T(2,128)S(1)} all-to-all(f32[64,2,256]{2,1,0:T(2,128)S(1)} %broadcast_in_dim.2), channel_id=1, replica_groups=mesh['yh'=2,'yl'=2,'x'=4,'zl'=2,'core'=2,'zh'=2] {'yh','yl','x','zl','co..., dimensions={0} | all-to-all | bytes 262144 | tf_op jit(solution)/shard_map/all_to_all | solution.py:82
  140.9 0.1 slice_reduce_fusion
  141.1 0.0 copy-done.2
  141.1 0.6 log_subtract_fusion
  141.7 0.8 multiply_convert_fusion
  (5 shorter events, 0.1 us)
Async XLA Ops:
  7.2 83.6 %all-gather.2.cloned.1.call-start = ((), (), s32[]{:S(2)}) async-start(), calls=%async_computation.1 | async-start | bytes 8650752 | tf_op jit(solution)/shard_map/all_gather | solution.py:57
  7.2 7.9 %collective-permute-start = (bf16[512,128]{1,0:T(8,128)(2,1)}, bf16[512,128]{1,0:T(8,128)(2,1)S(1)}, u32[]{:S(2)}, u32[]{:S(2)}) collective-permute-start(bf16[512,128]{1,0:T(8,128)(2,1)} %param.7), channel_id=1, source_target_pairs={{1,0},{64,65},{0,64},{65,1},{3,2},{66,67},{2,66},{67,3},{5,4},{68,... | collective-permute-start | bytes 393224 | tf_op jit(solution)/shard_map/ppermute | solution.py:51
  11.0 4.1 %collective-permute-start.1 = (bf16[512,128]{1,0:T(8,128)(2,1)}, bf16[512,128]{1,0:T(8,128)(2,1)S(1)}, u32[]{:S(2)}, u32[]{:S(2)}) collective-permute-start(bf16[512,128]{1,0:T(8,128)(2,1)} %param.7), channel_id=1, source_target_pairs={{1,64},{64,1},{3,66},{66,3},{5,68},{68,5},{7,70},{70,7},{9,72},{72... | collective-permute-start | bytes 393224 | tf_op jit(solution)/shard_map/ppermute | solution.py:52
  16.8 9.8 %collective-permute-start.2 = (bf16[256,256]{1,0:T(8,128)(2,1)}, bf16[256,256]{1,0:T(8,128)(2,1)S(1)}, u32[]{:S(2)}, u32[]{:S(2)}) collective-permute-start(bf16[256,256]{1,0:T(8,128)(2,1)} %param.8), channel_id=1, source_target_pairs={{0,1},{1,0},{2,3},{3,2},{4,5},{5,4},{6,7},{7,6},{8,9},{9,8},{10,11... | collective-permute-start | bytes 393224 | tf_op jit(solution)/shard_map/ppermute | solution.py:55
  106.5 18.3 %copy-start = (f32[512]{0:T(512)S(1)}, f32[512]{0:T(512)}, u32[]{:S(2)}) copy-start(f32[512]{0:T(512)} %param.9) | copy-start | bytes 6148
  106.5 18.3 %copy-start.1 = (f32[256]{0:T(256)S(1)}, f32[256]{0:T(256)}, u32[]{:S(2)}) copy-start(f32[256]{0:T(256)} %param.10) | copy-start | bytes 3076
  106.5 34.6 %copy-start.2 = (f32[256]{0:T(256)S(1)}, f32[256]{0:T(256)}, u32[]{:S(2)}) copy-start(f32[256]{0:T(256)} %param.11) | copy-start | bytes 3076
  106.5 18.2 %collective-permute-start.3 = (f32[512,256]{1,0:T(8,128)}, f32[512,256]{1,0:T(8,128)S(1)}, u32[]{:S(2)}, u32[]{:S(2)}) collective-permute-start(f32[512,256]{1,0:T(8,128)} %shard_map.78), channel_id=1, source_target_pairs={{0,1},{1,0},{2,3},{3,2},{4,5},{5,4},{6,7},{7,6},{8,9},{9,8},{10,11... | collective-permute-start | bytes 1572872 | tf_op jit(solution)/shard_map/ppermute | solution.py:71
Sparse Core Ops, SparseCore 0:
  17.0 73.7 all-gather.1

commit v6 on v4

--- a/solution.py
+++ b/solution.py
@@ -23,6 +23,7 @@
     holds = yh == zh
     piece = jnp.where(holds, jnp.concatenate([coupling, near], axis=1), jnp.concatenate([near, far], axis=1))
     second_x = lax.ppermute(dist_second, "zh", [(0, 1), (1, 0)])
+    piece, second_x = lax.optimization_barrier((piece, second_x))
 
     gathered = lax.all_gather(piece, GATHER, axis=0, tiled=True)
 

time: 142 us -> 142 us (level)
    all_gather x1, waiting for transfers between devices: 64 us -> 68 us  [body(): gathered = lax.all_gather(piece, GATHER, axis=0, tiled=True)]
    ppermute x1, waiting for transfers between devices: 3.44 us -> 0.01 us  [body(): lax.ppermute(coupling, ('yh', 'zh'), [(1, 0), (2, 3), (0, 2), (3, 1)])]
  transfers between devices with their start and end apart: 5 -> 5, of which waited for: 4 -> 3; matrix products, arithmetic and copies ran while one was open for 9% -> 10% of each run, Pallas kernels for 0% -> 0%
where the time goes in v6:
time: 142 us
  waiting for transfers between devices  69.5 us (49%)
  matrix products  23.4 us (16%)
  blocking collectives  15.7 us (11%)
  starting transfers between devices  14.6 us (10%)
  between operations  14.1 us (10%)
  other arithmetic  3.03 us (2%)
  local copies, waits for them, and re-layouts  1.85 us (1%)
    all_gather x1, waiting for transfers between devices, body(): gathered = lax.all_gather(piece, GATHER, axis=0, tiled=True)  68 us
    dot_general x2, matrix products, partial_gradient(): return jnp.dot(dist_first, product, preferred_element_type=jnp.float32)  23.4 us
    all_to_all x1, blocking collectives, body(): pairs = lax.all_to_all(copies, ROWS, 0, 0, tiled=True)  15.7 us
    ppermute x1, starting transfers between devices, body(): second_x = lax.ppermute(dist_second, 'zh', [(0, 1), (1, 0)])  7.6 us
    ppermute x1, starting transfers between devices, body(): lax.ppermute(coupling, ('yh', 'zh'), [(1, 0), (2, 3), (0, 2), (3, 1)])  3.81 us
  transfers between devices with their start and end apart: 5, of which 3 were waited for; matrix products, arithmetic and copies ran while one was open for 10% of the time, Pallas kernels for 0%

profile of v6, /device:TPU:1, one launch (start us, length us, event | category | flops | bytes accessed | tf_op | source)
XLA Modules:
  0.0 142.2 jit_solution(4111447625743902474)
XLA Ops:
  7.2 0.0 all-gather.2.cloned.1.call-start
  7.2 3.8 %collective-permute-start = (bf16[512,128]{1,0:T(8,128)(2,1)}, bf16[512,128]{1,0:T(8,128)(2,1)S(1)}, u32[]{:S(2)}, u32[]{:S(2)}) collective-permute-start(bf16[512,128]{1,0:T(8,128)(2,1)} %param.7), channel_id=1, source_target_pairs={{1,0},{64,65},{0,64},{65,1},{3,2},{66,67},{2,66},{67,3},{5,4},{68,... | collective-permute-start | bytes 393224 | tf_op jit(solution)/shard_map/ppermute | solution.py:21
  11.0 0.7 collective-permute-start.1
  11.7 7.6 %collective-permute-start.2 = (bf16[256,256]{1,0:T(8,128)(2,1)}, bf16[256,256]{1,0:T(8,128)(2,1)S(1)}, u32[]{:S(2)}, u32[]{:S(2)}) collective-permute-start(bf16[256,256]{1,0:T(8,128)(2,1)} %param.8), channel_id=1, source_target_pairs={{0,1},{1,0},{2,3},{3,2},{4,5},{5,4},{6,7},{7,6},{8,9},{9,8},{10,11... | collective-permute-start | bytes 393224 | tf_op jit(solution)/shard_map/ppermute | solution.py:25
  19.3 0.0 collective-permute-done
  19.3 0.0 collective-permute-done.1
  19.3 1.7 %maximum_select_fusion = bf16[512,256]{1,0:T(8,128)(2,1)} fusion(bf16[512,128]{1,0:T(8,128)(2,1)S(1)} %collective-permute-done, bf16[512,128]{1,0:T(8,128)(2,1)} %param.7, bf16[512,128]{1,0:T(8,128)(2,1)S(1)} %collective-permute-done.1, pred[]{:T(512)S(6)} %eq.3), kind=kLoop, calls=%fused_computation.9 | loop fusion | flops 1179648 | bytes 655361 | tf_op jit(solution)/shard_map/jit(_where)/select_n | solution.py:24
  21.0 0.9 collective-permute-done.2
  21.9 0.0 all-gather.2.cloned.1.call-update
  21.9 0.9 constant_dynamic-update-slice_fusion.1
  22.9 68.0 %all-gather.2.cloned.1.call-done = bf16[16384,256]{1,0:T(8,128)(2,1)} async-done(((bf16[512,256]{1,0:T(8,128)(2,1)}), bf16[16384,256]{1,0:T(8,128)(2,1)}) %all-gather.2.cloned.1.call-update) | async-done | bytes 8388624 | tf_op jit(solution)/shard_map/all_gather | solution.py:28
  90.9 11.7 %fusion.2 = f32[512,256]{0,1:T(8,128)S(1)} fusion(bf16[512,16384]{1,0:T(8,128)(2,1)} %param.6, bf16[16384,256]{1,0:T(8,128)(2,1)} %all-gather.2.cloned.1.call-done, bf16[128,512]{1,0:T(8,128)(2,1)S(1)} %get-tuple-element.18, bf16[128,512]{1,0:T(8,128)(2,1)S(1)} %get-tuple-element.19), kind=kOutput, calls=%fused_computation.4 | convolution fusion | flops 6446907392 | bytes 25952256 | tf_op jit(solution)/shard_map/dot_general | solution.py:42
  102.5 0.0 copy-start
  102.6 0.0 copy-start.1
  102.6 0.0 copy-start.2
  102.6 2.5 %collective-permute-start.3 = (f32[512,256]{0,1:T(8,128)S(1)}, f32[512,256]{0,1:T(8,128)S(1)}, u32[]{:S(2)}, u32[]{:S(2)}) collective-permute-start(f32[512,256]{0,1:T(8,128)S(1)} %fusion.2), channel_id=1, source_target_pairs={{0,1},{1,0},{2,3},{3,2},{4,5},{5,4},{6,7},{7,6},{8,9},{9,8},{10,11... | collective-permute-start | bytes 1572872 | tf_op jit(solution)/shard_map/ppermute | solution.py:45
  105.1 11.7 %fusion.3 = f32[512,256]{0,1:T(8,128)S(1)} fusion(bf16[512,16384]{1,0:T(8,128)(2,1)} %param.6, bf16[16384,256]{1,0:T(8,128)(2,1)} %all-gather.2.cloned.1.call-done, bf16[128,512]{1,0:T(8,128)(2,1)S(1)} %get-tuple-element.19, bf16[128,512]{1,0:T(8,128)(2,1)S(1)} %get-tuple-element.18), kind=kOutput, calls=%fused_computation.5 | convolution fusion | flops 6446907392 | bytes 25952256 | tf_op jit(solution)/shard_map/dot_general | solution.py:42
  116.8 0.6 collective-permute-done.3
  117.4 0.0 copy-done
  117.4 0.0 copy-done.1
  117.4 0.2 fusion.17
  117.6 0.2 exponential_reduce_fusion
  117.9 15.7 %all_to_all.5 = f32[64,2,256]{2,1,0:T(2,128)S(1)} all-to-all(f32[64,2,256]{2,1,0:T(2,128)S(1)} %broadcast_in_dim.2), channel_id=1, replica_groups=mesh['yh'=2,'yl'=2,'x'=4,'zl'=2,'core'=2,'zh'=2] {'yh','yl','x','zl','co..., dimensions={0} | all-to-all | bytes 262144 | tf_op jit(solution)/shard_map/all_to_all | solution.py:56
  133.6 0.1 slice_reduce_fusion
  133.8 0.0 copy-done.2
  133.8 0.6 log_subtract_fusion
  134.3 0.1 multiply_convert_fusion
  134.5 0.8 copy.12
  (5 shorter events, 0.1 us)
Async XLA Ops:
  7.2 83.7 %all-gather.2.cloned.1.call-start = ((), (), s32[]{:S(2)}) async-start(), calls=%async_computation.1 | async-start | bytes 8650752 | tf_op jit(solution)/shard_map/all_gather | solution.py:28
  7.2 12.1 %collective-permute-start = (bf16[512,128]{1,0:T(8,128)(2,1)}, bf16[512,128]{1,0:T(8,128)(2,1)S(1)}, u32[]{:S(2)}, u32[]{:S(2)}) collective-permute-start(bf16[512,128]{1,0:T(8,128)(2,1)} %param.7), channel_id=1, source_target_pairs={{1,0},{64,65},{0,64},{65,1},{3,2},{66,67},{2,66},{67,3},{5,4},{68,... | collective-permute-start | bytes 393224 | tf_op jit(solution)/shard_map/ppermute | solution.py:21
  11.0 8.3 %collective-permute-start.1 = (bf16[512,128]{1,0:T(8,128)(2,1)}, bf16[512,128]{1,0:T(8,128)(2,1)S(1)}, u32[]{:S(2)}, u32[]{:S(2)}) collective-permute-start(bf16[512,128]{1,0:T(8,128)(2,1)} %param.7), channel_id=1, source_target_pairs={{1,64},{64,1},{3,66},{66,3},{5,68},{68,5},{7,70},{70,7},{9,72},{72... | collective-permute-start | bytes 393224 | tf_op jit(solution)/shard_map/ppermute | solution.py:22
  11.7 10.2 %collective-permute-start.2 = (bf16[256,256]{1,0:T(8,128)(2,1)}, bf16[256,256]{1,0:T(8,128)(2,1)S(1)}, u32[]{:S(2)}, u32[]{:S(2)}) collective-permute-start(bf16[256,256]{1,0:T(8,128)(2,1)} %param.8), channel_id=1, source_target_pairs={{0,1},{1,0},{2,3},{3,2},{4,5},{5,4},{6,7},{7,6},{8,9},{9,8},{10,11... | collective-permute-start | bytes 393224 | tf_op jit(solution)/shard_map/ppermute | solution.py:25
  102.5 14.9 %copy-start = (f32[512]{0:T(512)S(1)}, f32[512]{0:T(512)}, u32[]{:S(2)}) copy-start(f32[512]{0:T(512)} %param.9) | copy-start | bytes 6148
  102.6 14.8 %copy-start.1 = (f32[256]{0:T(256)S(1)}, f32[256]{0:T(256)}, u32[]{:S(2)}) copy-start(f32[256]{0:T(256)} %param.10) | copy-start | bytes 3076
  102.6 31.2 %copy-start.2 = (f32[256]{0:T(256)S(1)}, f32[256]{0:T(256)}, u32[]{:S(2)}) copy-start(f32[256]{0:T(256)} %param.11) | copy-start | bytes 3076
  102.6 14.8 %collective-permute-start.3 = (f32[512,256]{0,1:T(8,128)S(1)}, f32[512,256]{0,1:T(8,128)S(1)}, u32[]{:S(2)}, u32[]{:S(2)}) collective-permute-start(f32[512,256]{0,1:T(8,128)S(1)} %fusion.2), channel_id=1, source_target_pairs={{0,1},{1,0},{2,3},{3,2},{4,5},{5,4},{6,7},{7,6},{8,9},{9,8},{10,11... | collective-permute-start | bytes 1572872 | tf_op jit(solution)/shard_map/ppermute | solution.py:45
Sparse Core Ops, SparseCore 0:
  22.0 68.8 all-gather.1

commit v7 on v4

--- a/solution.py
+++ b/solution.py
@@ -8,7 +8,6 @@
 N = 32768
 AXES = ("yh", "yl", "x", "zl", "core", "zh")
 ROWS = ("yh", "yl", "x", "zl", "core")
-GATHER = ("yl", "x", "zl", "core")
 
 
 def body(dist_first, coupling, dist_second, row_potential, column_cost, column_mass):
@@ -24,7 +23,10 @@
     piece = jnp.where(holds, jnp.concatenate([coupling, near], axis=1), jnp.concatenate([near, far], axis=1))
     second_x = lax.ppermute(dist_second, "zh", [(0, 1), (1, 0)])
 
-    gathered = lax.all_gather(piece, GATHER, axis=0, tiled=True)
+    pair_rows = lax.all_gather(piece, "yl", axis=0, tiled=True)
+    gathered = lax.all_gather(pair_rows, ("x", "zl", "core"), axis=0, tiled=True)
+    gathered = gathered.reshape(4, 2, 2, 2, blocks, 2 * k_half)
+    gathered = jnp.transpose(gathered, (3, 0, 1, 2, 4, 5)).reshape(-1, 2 * k_half)
 
     second_full = jnp.concatenate([dist_second, second_x], axis=1)
     second_k = jnp.concatenate(

time: 142 us -> 144 us (1.014)
  waiting for transfers between devices: 69.8 us -> 55.9 us
  blocking collectives: 15.7 us -> 24.5 us
  local copies, waits for them, and re-layouts: 1.88 us -> 9.37 us
    all_gather x1, waiting for transfers between devices: 64 us -> 50.4 us  [body(): lax.all_gather(pair_rows, ('x', 'zl', 'core'), axis=0, tiled=True)]
    transpose x0 -> x1, local copies, waits for them, and re-layouts: none -> 7.48 us  [body(): jnp.transpose(gathered, (3, 0, 1, 2, 4, 5)).reshape(-1, 2 * k_half)]
    all_gather x0 -> x1, blocking collectives: none -> 7.35 us  [body(): pair_rows = lax.all_gather(piece, 'yl', axis=0, tiled=True)]
    all_to_all x1, blocking collectives: 15.7 us -> 17.1 us  [body(): pairs = lax.all_to_all(copies, ROWS, 0, 0, tiled=True)]
where the time goes in v7:
time: 144 us
  waiting for transfers between devices  55.9 us (39%)
  blocking collectives  24.5 us (17%)
  matrix products  23.4 us (16%)
  starting transfers between devices  14.2 us (10%)
  between operations  14.1 us (10%)
  local copies, waits for them, and re-layouts  9.37 us (7%)
  other arithmetic  2.32 us (2%)
    all_gather x1, waiting for transfers between devices, body(): lax.all_gather(pair_rows, ('x', 'zl', 'core'), axis=0, tiled=True)  50.4 us
    dot_general x2, matrix products, partial_gradient(): return jnp.dot(dist_first, product, preferred_element_type=jnp.float32)  23.4 us
    all_to_all x1, blocking collectives, body(): pairs = lax.all_to_all(copies, ROWS, 0, 0, tiled=True)  17.1 us
    transpose x1, local copies, waits for them, and re-layouts, body(): jnp.transpose(gathered, (3, 0, 1, 2, 4, 5)).reshape(-1, 2 * k_half)  7.48 us
    all_gather x1, blocking collectives, body(): pair_rows = lax.all_gather(piece, 'yl', axis=0, tiled=True)  7.35 us
    ppermute x1, starting transfers between devices, body(): second_x = lax.ppermute(dist_second, 'zh', [(0, 1), (1, 0)])  6.93 us
    ppermute x1, starting transfers between devices, body(): lax.ppermute(coupling, ('yh', 'zh'), [(1, 0), (2, 3), (0, 2), (3, 1)])  3.81 us
    ppermute x1, waiting for transfers between devices, body(): lax.ppermute(coupling, ('yh', 'zh'), [(1, 0), (2, 3), (0, 2), (3, 1)])  3.44 us
  transfers between devices with their start and end apart: 5, of which 4 were waited for; matrix products, arithmetic and copies ran while one was open for 9% of the time, Pallas kernels for 0%

profile of v7, /device:TPU:1, one launch (start us, length us, event | category | flops | bytes accessed | tf_op | source)
XLA Modules:
  0.0 143.7 jit_solution(518701083949521681)
XLA Ops:
  7.2 0.0 all-gather.2.cloned.1.call-start
  7.2 3.8 %collective-permute-start = (bf16[512,128]{1,0:T(8,128)(2,1)}, bf16[512,128]{1,0:T(8,128)(2,1)S(1)}, u32[]{:S(2)}, u32[]{:S(2)}) collective-permute-start(bf16[512,128]{1,0:T(8,128)(2,1)} %param.7), channel_id=1, source_target_pairs={{1,0},{64,65},{0,64},{65,1},{3,2},{66,67},{2,66},{67,3},{5,4},{68,... | collective-permute-start | bytes 393224 | tf_op jit(solution)/shard_map/ppermute | solution.py:20
  11.0 0.7 collective-permute-start.1
  11.7 3.4 %collective-permute-done = bf16[512,128]{1,0:T(8,128)(2,1)S(1)} collective-permute-done((bf16[512,128]{1,0:T(8,128)(2,1)}, bf16[512,128]{1,0:T(8,128)(2,1)S(1)}, u32[]{:S(2)}, u32[]{:S(2)}) %collective-permute-start) | collective-permute-done | bytes 131104 | tf_op jit(solution)/shard_map/ppermute | solution.py:20
  15.1 0.0 collective-permute-done.1
  15.1 1.0 maximum_select_fusion
  16.1 7.3 %all_gather.6 = bf16[1024,256]{1,0:T(8,128)(2,1)} all-gather(bf16[512,256]{1,0:T(8,128)(2,1)S(1)} %maximum_select_fusion), channel_id=1, replica_groups=mesh['yh'=2,'yl'=2,'x'=4,'zl'=2,'core'=2,'zh'=2] {'yl'}, dimensions={0}, use_global_device_ids=true | all-gather | bytes 786432 | tf_op jit(solution)/shard_map/all_gather | solution.py:26
  23.5 0.0 all-gather.2.cloned.1.call-update
  23.5 6.9 %collective-permute-start.2 = (bf16[256,256]{1,0:T(8,128)(2,1)}, bf16[256,256]{1,0:T(8,128)(2,1)S(1)}, u32[]{:S(2)}, u32[]{:S(2)}) collective-permute-start(bf16[256,256]{1,0:T(8,128)(2,1)} %param.8), channel_id=1, source_target_pairs={{0,1},{1,0},{2,3},{3,2},{4,5},{5,4},{6,7},{7,6},{8,9},{9,8},{10,11... | collective-permute-start | bytes 393224 | tf_op jit(solution)/shard_map/ppermute | solution.py:24
  30.4 0.9 constant_dynamic-update-slice_fusion.1
  31.4 1.6 %collective-permute-done.2 = bf16[256,256]{1,0:T(8,128)(2,1)S(1)} collective-permute-done((bf16[256,256]{1,0:T(8,128)(2,1)}, bf16[256,256]{1,0:T(8,128)(2,1)S(1)}, u32[]{:S(2)}, u32[]{:S(2)}) %collective-permute-start.2) | collective-permute-done | bytes 131104 | tf_op jit(solution)/shard_map/ppermute | solution.py:24
  33.1 50.4 %all-gather.2.cloned.1.call-done = bf16[16384,256]{1,0:T(8,128)(2,1)} async-done(((bf16[1024,256]{1,0:T(8,128)(2,1)}), bf16[16384,256]{1,0:T(8,128)(2,1)}) %all-gather.2.cloned.1.call-update) | async-done | bytes 8388624 | tf_op jit(solution)/shard_map/all_gather | solution.py:27
  83.5 7.5 %copy.17 = bf16[2,4,2,2,512,256]{5,4,3,2,1,0:T(8,128)(2,1)} copy(bf16[2,4,2,2,512,256]{5,4,0,3,2,1:T(8,128)(2,1)} %bitcast.26) | data formatting | bytes 16777216 | tf_op jit(solution)/shard_map/transpose | solution.py:29
  90.9 11.7 %fusion.2 = f32[512,256]{0,1:T(8,128)S(1)} fusion(bf16[512,16384]{1,0:T(8,128)(2,1)} %param.6, bf16[16384,256]{1,0:T(8,128)(2,1)} %bitcast.27, bf16[128,512]{1,0:T(8,128)(2,1)S(1)} %get-tuple-element.18, bf16[128,512]{1,0:T(8,128)(2,1)S(1)} %get-tuple-element.19), kind=kOutput, calls=%fused_computation.4 | convolution fusion | flops 6446907392 | bytes 25952256 | tf_op jit(solution)/shard_map/dot_general | solution.py:43
  102.6 0.0 copy-start
  102.6 0.0 copy-start.1
  102.7 0.0 copy-start.2
  102.7 2.8 %collective-permute-start.3 = (f32[512,256]{0,1:T(8,128)S(1)}, f32[512,256]{0,1:T(8,128)S(1)}, u32[]{:S(2)}, u32[]{:S(2)}) collective-permute-start(f32[512,256]{0,1:T(8,128)S(1)} %fusion.2), channel_id=1, source_target_pairs={{0,1},{1,0},{2,3},{3,2},{4,5},{5,4},{6,7},{7,6},{8,9},{9,8},{10,11... | collective-permute-start | bytes 1572872 | tf_op jit(solution)/shard_map/ppermute | solution.py:46
  105.4 11.7 %fusion.3 = f32[512,256]{0,1:T(8,128)S(1)} fusion(bf16[512,16384]{1,0:T(8,128)(2,1)} %param.6, bf16[16384,256]{1,0:T(8,128)(2,1)} %bitcast.28, bf16[128,512]{1,0:T(8,128)(2,1)S(1)} %get-tuple-element.19, bf16[128,512]{1,0:T(8,128)(2,1)S(1)} %get-tuple-element.18), kind=kOutput, calls=%fused_computation.5 | convolution fusion | flops 6446907392 | bytes 25952256 | tf_op jit(solution)/shard_map/dot_general | solution.py:43
  117.1 0.4 collective-permute-done.3
  117.5 0.0 copy-done
  117.5 0.0 copy-done.1
  117.5 0.2 fusion.17
  117.7 0.2 exponential_reduce_fusion
  118.0 17.1 %all_to_all.5 = f32[64,2,256]{2,1,0:T(2,128)S(1)} all-to-all(f32[64,2,256]{2,1,0:T(2,128)S(1)} %broadcast_in_dim.2), channel_id=1, replica_groups=mesh['yh'=2,'yl'=2,'x'=4,'zl'=2,'core'=2,'zh'=2] {'yh','yl','x','zl','co..., dimensions={0} | all-to-all | bytes 262144 | tf_op jit(solution)/shard_map/all_to_all | solution.py:57
  135.1 0.1 slice_reduce_fusion
  135.3 0.0 copy-done.2
  135.3 0.6 log_subtract_fusion
  135.9 0.1 multiply_convert_fusion
  136.0 0.8 copy.19
  (5 shorter events, 0.1 us)
Async XLA Ops:
  7.2 76.3 %all-gather.2.cloned.1.call-start = ((), (), s32[]{:S(2)}) async-start(), calls=%async_computation.1 | async-start | bytes 8912896 | tf_op jit(solution)/shard_map/all_gather | solution.py:27
  7.2 7.9 %collective-permute-start = (bf16[512,128]{1,0:T(8,128)(2,1)}, bf16[512,128]{1,0:T(8,128)(2,1)S(1)}, u32[]{:S(2)}, u32[]{:S(2)}) collective-permute-start(bf16[512,128]{1,0:T(8,128)(2,1)} %param.7), channel_id=1, source_target_pairs={{1,0},{64,65},{0,64},{65,1},{3,2},{66,67},{2,66},{67,3},{5,4},{68,... | collective-permute-start | bytes 393224 | tf_op jit(solution)/shard_map/ppermute | solution.py:20
  11.0 4.1 %collective-permute-start.1 = (bf16[512,128]{1,0:T(8,128)(2,1)}, bf16[512,128]{1,0:T(8,128)(2,1)S(1)}, u32[]{:S(2)}, u32[]{:S(2)}) collective-permute-start(bf16[512,128]{1,0:T(8,128)(2,1)} %param.7), channel_id=1, source_target_pairs={{1,64},{64,1},{3,66},{66,3},{5,68},{68,5},{7,70},{70,7},{9,72},{72... | collective-permute-start | bytes 393224 | tf_op jit(solution)/shard_map/ppermute | solution.py:21
  23.5 9.5 %collective-permute-start.2 = (bf16[256,256]{1,0:T(8,128)(2,1)}, bf16[256,256]{1,0:T(8,128)(2,1)S(1)}, u32[]{:S(2)}, u32[]{:S(2)}) collective-permute-start(bf16[256,256]{1,0:T(8,128)(2,1)} %param.8), channel_id=1, source_target_pairs={{0,1},{1,0},{2,3},{3,2},{4,5},{5,4},{6,7},{7,6},{8,9},{9,8},{10,11... | collective-permute-start | bytes 393224 | tf_op jit(solution)/shard_map/ppermute | solution.py:24
  102.6 14.9 %copy-start = (f32[512]{0:T(512)S(1)}, f32[512]{0:T(512)}, u32[]{:S(2)}) copy-start(f32[512]{0:T(512)} %param.9) | copy-start | bytes 6148
  102.6 14.9 %copy-start.1 = (f32[256]{0:T(256)S(1)}, f32[256]{0:T(256)}, u32[]{:S(2)}) copy-start(f32[256]{0:T(256)} %param.10) | copy-start | bytes 3076
  102.7 32.7 %copy-start.2 = (f32[256]{0:T(256)S(1)}, f32[256]{0:T(256)}, u32[]{:S(2)}) copy-start(f32[256]{0:T(256)} %param.11) | copy-start | bytes 3076
  102.7 14.8 %collective-permute-start.3 = (f32[512,256]{0,1:T(8,128)S(1)}, f32[512,256]{0,1:T(8,128)S(1)}, u32[]{:S(2)}, u32[]{:S(2)}) collective-permute-start(f32[512,256]{0,1:T(8,128)S(1)} %fusion.2), channel_id=1, source_target_pairs={{0,1},{1,0},{2,3},{3,2},{4,5},{5,4},{6,7},{7,6},{8,9},{9,8},{10,11... | collective-permute-start | bytes 1572872 | tf_op jit(solution)/shard_map/ppermute | solution.py:46
Sparse Core Ops, SparseCore 0:
  23.6 59.7 all-gather.1

commit v8 on v7

--- a/solution.py
+++ b/solution.py
@@ -19,12 +19,32 @@
 
     near = lax.ppermute(coupling, ("yh", "zh"), [(1, 0), (2, 3), (0, 2), (3, 1)])
     far = lax.ppermute(coupling, ("yh", "zh"), [(1, 2), (2, 1)])
+    def at(a, b, c):
+        return a * 4 + b * 2 + c
+
+    first_pairs, second_pairs = [], []
+    for a in range(2):
+        for b in range(2):
+            first_pairs += [(at(a, b, a), at(a, 1 - b, a)), (at(a, b, 1 - a), at(1 - a, 1 - b, a))]
+            second_pairs += [(at(a, b, a), at(1 - a, 1 - b, a)), (at(a, b, 1 - a), at(a, 1 - b, a))]
+    other_first = lax.ppermute(coupling, ("yh", "yl", "zh"), first_pairs)
+    other_second = lax.ppermute(coupling, ("yh", "yl", "zh"), second_pairs)
     holds = yh == zh
-    piece = jnp.where(holds, jnp.concatenate([coupling, near], axis=1), jnp.concatenate([near, far], axis=1))
+    own_block = jnp.where(holds, jnp.concatenate([coupling, near], axis=1), jnp.concatenate([near, far], axis=1))
+    other_block = jnp.where(
+        holds,
+        jnp.concatenate([other_first, other_second], axis=1),
+        jnp.concatenate([other_second, other_first], axis=1),
+    )
+    yl = lax.axis_index("yl")
+    piece = jnp.where(
+        yl == 0,
+        jnp.concatenate([own_block, other_block], axis=0),
+        jnp.concatenate([other_block, own_block], axis=0),
+    )
     second_x = lax.ppermute(dist_second, "zh", [(0, 1), (1, 0)])
 
-    pair_rows = lax.all_gather(piece, "yl", axis=0, tiled=True)
-    gathered = lax.all_gather(pair_rows, ("x", "zl", "core"), axis=0, tiled=True)
+    gathered = lax.all_gather(piece, ("x", "zl", "core"), axis=0, tiled=True)
     gathered = gathered.reshape(4, 2, 2, 2, blocks, 2 * k_half)
     gathered = jnp.transpose(gathered, (3, 0, 1, 2, 4, 5)).reshape(-1, 2 * k_half)
 

time: 144 us -> 140 us (0.972)
  blocking collectives: 24.5 us -> 17.1 us
  starting transfers between devices: 14.2 us -> 18.9 us
  waiting for transfers between devices: 55.9 us -> 53.8 us
    all_gather x1 -> x0, blocking collectives: 7.35 us -> none  [body(): pair_rows = lax.all_gather(piece, 'yl', axis=0, tiled=True)]
    ppermute x0 -> x2, starting transfers between devices: none -> 3.64 us  [the longest x1 3.63 us: body(): other_second = lax.ppermute(coupling, ('yh', 'yl', 'zh'), second_pairs)]
    all_gather x1, waiting for transfers between devices: 50.4 us -> 48 us  [body(): gathered = lax.all_gather(piece, ('x', 'zl', 'core'), axis=0, tiled=True)]
  transfers between devices with their start and end apart: 5 -> 7, of which waited for: 4 -> 5; matrix products, arithmetic and copies ran while one was open for 9% -> 9% of each run, Pallas kernels for 0% -> 0%
where the time goes in v8:
time: 140 us
  waiting for transfers between devices  53.8 us (38%)
  matrix products  23.4 us (17%)
  starting transfers between devices  18.9 us (13%)
  blocking collectives  17.1 us (12%)
  between operations  14.1 us (10%)
  local copies, waits for them, and re-layouts  9.36 us (7%)
  other arithmetic  3.49 us (2%)
    all_gather x1, waiting for transfers between devices, body(): gathered = lax.all_gather(piece, ('x', 'zl', 'core'), axis=0, tiled=True)  48 us
    dot_general x2, matrix products, partial_gradient(): return jnp.dot(dist_first, product, preferred_element_type=jnp.float32)  23.4 us
    all_to_all x1, blocking collectives, body(): pairs = lax.all_to_all(copies, ROWS, 0, 0, tiled=True)  17.1 us
    transpose x1, local copies, waits for them, and re-layouts, body(): jnp.transpose(gathered, (3, 0, 1, 2, 4, 5)).reshape(-1, 2 * k_half)  7.47 us
    ppermute x1, starting transfers between devices, body(): second_x = lax.ppermute(dist_second, 'zh', [(0, 1), (1, 0)])  7.3 us
    ppermute x1, starting transfers between devices, body(): lax.ppermute(coupling, ('yh', 'zh'), [(1, 0), (2, 3), (0, 2), (3, 1)])  4.5 us
    ppermute x1, waiting for transfers between devices, body(): lax.ppermute(coupling, ('yh', 'zh'), [(1, 0), (2, 3), (0, 2), (3, 1)])  3.66 us
    ppermute x1, starting transfers between devices, body(): other_second = lax.ppermute(coupling, ('yh', 'yl', 'zh'), second_pairs)  3.63 us
  transfers between devices with their start and end apart: 7, of which 5 were waited for; matrix products, arithmetic and copies ran while one was open for 9% of the time, Pallas kernels for 0%

profile of v8, /device:TPU:1, one launch (start us, length us, event | category | flops | bytes accessed | tf_op | source)
XLA Modules:
  0.0 140.2 jit_solution(17151147743597879517)
XLA Ops:
  7.2 0.0 all-gather.2.cloned.1.call-start
  7.2 3.6 %collective-permute-start.3 = (bf16[512,128]{1,0:T(8,128)(2,1)}, bf16[512,128]{1,0:T(8,128)(2,1)S(1)}, u32[]{:S(2)}, u32[]{:S(2)}) collective-permute-start(bf16[512,128]{1,0:T(8,128)(2,1)} %param.7), channel_id=1, source_target_pairs={{0,96},{1,32},{32,64},{33,0},{65,33},{64,97},{97,1},{96,65},{2,98}... | collective-permute-start | bytes 393224 | tf_op jit(solution)/shard_map/ppermute | solution.py:31
  10.8 0.0 collective-permute-start.2
  10.8 4.5 %collective-permute-start = (bf16[512,128]{1,0:T(8,128)(2,1)}, bf16[512,128]{1,0:T(8,128)(2,1)S(1)}, u32[]{:S(2)}, u32[]{:S(2)}) collective-permute-start(bf16[512,128]{1,0:T(8,128)(2,1)} %param.7), channel_id=1, source_target_pairs={{1,0},{64,65},{0,64},{65,1},{3,2},{66,67},{2,66},{67,3},{5,4},{68,... | collective-permute-start | bytes 393224 | tf_op jit(solution)/shard_map/ppermute | solution.py:20
  15.3 0.7 collective-permute-start.1
  16.0 0.1 collective-permute-done.3
  16.2 0.0 collective-permute-done.2
  16.2 0.1 maximum_select_fusion.2
  16.2 3.7 %collective-permute-done = bf16[512,128]{1,0:T(8,128)(2,1)S(1)} collective-permute-done((bf16[512,128]{1,0:T(8,128)(2,1)}, bf16[512,128]{1,0:T(8,128)(2,1)S(1)}, u32[]{:S(2)}, u32[]{:S(2)}) %collective-permute-start) | collective-permute-done | bytes 131104 | tf_op jit(solution)/shard_map/ppermute | solution.py:20
  19.9 0.0 collective-permute-done.1
  19.9 1.0 maximum_select_fusion.1
  20.9 1.1 maximum_select_fusion
  22.0 0.0 all-gather.2.cloned.1.call-update
  22.0 7.3 %collective-permute-start.4 = (bf16[256,256]{1,0:T(8,128)(2,1)}, bf16[256,256]{1,0:T(8,128)(2,1)S(1)}, u32[]{:S(2)}, u32[]{:S(2)}) collective-permute-start(bf16[256,256]{1,0:T(8,128)(2,1)} %param.8), channel_id=1, source_target_pairs={{0,1},{1,0},{2,3},{3,2},{4,5},{5,4},{6,7},{7,6},{8,9},{9,8},{10,11... | collective-permute-start | bytes 393224 | tf_op jit(solution)/shard_map/ppermute | solution.py:45
  29.3 0.9 constant_dynamic-update-slice_fusion.1
  30.2 1.6 %collective-permute-done.4 = bf16[256,256]{1,0:T(8,128)(2,1)S(1)} collective-permute-done((bf16[256,256]{1,0:T(8,128)(2,1)}, bf16[256,256]{1,0:T(8,128)(2,1)S(1)}, u32[]{:S(2)}, u32[]{:S(2)}) %collective-permute-start.4) | collective-permute-done | bytes 131104 | tf_op jit(solution)/shard_map/ppermute | solution.py:45
  31.9 48.0 %all-gather.2.cloned.1.call-done = bf16[16384,256]{1,0:T(8,128)(2,1)} async-done(((bf16[1024,256]{1,0:T(8,128)(2,1)}), bf16[16384,256]{1,0:T(8,128)(2,1)}) %all-gather.2.cloned.1.call-update) | async-done | bytes 8388624 | tf_op jit(solution)/shard_map/all_gather | solution.py:47
  79.9 7.5 %copy.17 = bf16[2,4,2,2,512,256]{5,4,3,2,1,0:T(8,128)(2,1)} copy(bf16[2,4,2,2,512,256]{5,4,0,3,2,1:T(8,128)(2,1)} %bitcast.26) | data formatting | bytes 16777216 | tf_op jit(solution)/shard_map/transpose | solution.py:49
  87.4 11.7 %fusion.2 = f32[512,256]{0,1:T(8,128)S(1)} fusion(bf16[512,16384]{1,0:T(8,128)(2,1)} %param.6, bf16[16384,256]{1,0:T(8,128)(2,1)} %bitcast.27, bf16[128,512]{1,0:T(8,128)(2,1)S(1)} %get-tuple-element.18, bf16[128,512]{1,0:T(8,128)(2,1)S(1)} %get-tuple-element.19), kind=kOutput, calls=%fused_computation.4 | convolution fusion | flops 6446907392 | bytes 25952256 | tf_op jit(solution)/shard_map/dot_general | solution.py:63
  99.1 0.0 copy-start
  99.1 0.0 copy-start.1
  99.1 0.0 copy-start.2
  99.1 2.8 %collective-permute-start.5 = (f32[512,256]{0,1:T(8,128)S(1)}, f32[512,256]{0,1:T(8,128)S(1)}, u32[]{:S(2)}, u32[]{:S(2)}) collective-permute-start(f32[512,256]{0,1:T(8,128)S(1)} %fusion.2), channel_id=1, source_target_pairs={{0,1},{1,0},{2,3},{3,2},{4,5},{5,4},{6,7},{7,6},{8,9},{9,8},{10,11... | collective-permute-start | bytes 1572872 | tf_op jit(solution)/shard_map/ppermute | solution.py:66
  101.9 11.7 %fusion.3 = f32[512,256]{0,1:T(8,128)S(1)} fusion(bf16[512,16384]{1,0:T(8,128)(2,1)} %param.6, bf16[16384,256]{1,0:T(8,128)(2,1)} %bitcast.28, bf16[128,512]{1,0:T(8,128)(2,1)S(1)} %get-tuple-element.19, bf16[128,512]{1,0:T(8,128)(2,1)S(1)} %get-tuple-element.18), kind=kOutput, calls=%fused_computation.5 | convolution fusion | flops 6446907392 | bytes 25952256 | tf_op jit(solution)/shard_map/dot_general | solution.py:63
  113.6 0.4 collective-permute-done.5
  114.0 0.2 fusion.17
  114.2 0.2 exponential_reduce_fusion
  114.5 17.1 %all_to_all.5 = f32[64,2,256]{2,1,0:T(2,128)S(1)} all-to-all(f32[64,2,256]{2,1,0:T(2,128)S(1)} %broadcast_in_dim.2), channel_id=1, replica_groups=mesh['yh'=2,'yl'=2,'x'=4,'zl'=2,'core'=2,'zh'=2] {'yh','yl','x','zl','co..., dimensions={0} | all-to-all | bytes 262144 | tf_op jit(solution)/shard_map/all_to_all | solution.py:77
  131.6 0.1 slice_reduce_fusion
  131.8 0.6 log_subtract_fusion
  132.4 0.1 multiply_convert_fusion
  132.5 0.8 copy.19
  (8 shorter events, 0.1 us)
Async XLA Ops:
  7.2 72.8 %all-gather.2.cloned.1.call-start = ((), (), s32[]{:S(2)}) async-start(), calls=%async_computation.1 | async-start | bytes 8912896 | tf_op jit(solution)/shard_map/all_gather | solution.py:47
  7.2 8.9 %collective-permute-start.3 = (bf16[512,128]{1,0:T(8,128)(2,1)}, bf16[512,128]{1,0:T(8,128)(2,1)S(1)}, u32[]{:S(2)}, u32[]{:S(2)}) collective-permute-start(bf16[512,128]{1,0:T(8,128)(2,1)} %param.7), channel_id=1, source_target_pairs={{0,96},{1,32},{32,64},{33,0},{65,33},{64,97},{97,1},{96,65},{2,98}... | collective-permute-start | bytes 393224 | tf_op jit(solution)/shard_map/ppermute | solution.py:31
  10.8 5.3 %collective-permute-start.2 = (bf16[512,128]{1,0:T(8,128)(2,1)}, bf16[512,128]{1,0:T(8,128)(2,1)S(1)}, u32[]{:S(2)}, u32[]{:S(2)}) collective-permute-start(bf16[512,128]{1,0:T(8,128)(2,1)} %param.7), channel_id=1, source_target_pairs={{0,32},{1,96},{32,0},{33,64},{65,97},{64,33},{97,65},{96,1},{2,34}... | collective-permute-start | bytes 393224 | tf_op jit(solution)/shard_map/ppermute | solution.py:30
  10.8 9.1 %collective-permute-start = (bf16[512,128]{1,0:T(8,128)(2,1)}, bf16[512,128]{1,0:T(8,128)(2,1)S(1)}, u32[]{:S(2)}, u32[]{:S(2)}) collective-permute-start(bf16[512,128]{1,0:T(8,128)(2,1)} %param.7), channel_id=1, source_target_pairs={{1,0},{64,65},{0,64},{65,1},{3,2},{66,67},{2,66},{67,3},{5,4},{68,... | collective-permute-start | bytes 393224 | tf_op jit(solution)/shard_map/ppermute | solution.py:20
  15.3 4.6 %collective-permute-start.1 = (bf16[512,128]{1,0:T(8,128)(2,1)}, bf16[512,128]{1,0:T(8,128)(2,1)S(1)}, u32[]{:S(2)}, u32[]{:S(2)}) collective-permute-start(bf16[512,128]{1,0:T(8,128)(2,1)} %param.7), channel_id=1, source_target_pairs={{1,64},{64,1},{3,66},{66,3},{5,68},{68,5},{7,70},{70,7},{9,72},{72... | collective-permute-start | bytes 393224 | tf_op jit(solution)/shard_map/ppermute | solution.py:21
  22.0 9.9 %collective-permute-start.4 = (bf16[256,256]{1,0:T(8,128)(2,1)}, bf16[256,256]{1,0:T(8,128)(2,1)S(1)}, u32[]{:S(2)}, u32[]{:S(2)}) collective-permute-start(bf16[256,256]{1,0:T(8,128)(2,1)} %param.8), channel_id=1, source_target_pairs={{0,1},{1,0},{2,3},{3,2},{4,5},{5,4},{6,7},{7,6},{8,9},{9,8},{10,11... | collective-permute-start | bytes 393224 | tf_op jit(solution)/shard_map/ppermute | solution.py:45
  99.1 14.9 %copy-start = (f32[512]{0:T(512)S(1)}, f32[512]{0:T(512)}, u32[]{:S(2)}) copy-start(f32[512]{0:T(512)} %param.9) | copy-start | bytes 6148
  99.1 14.9 %copy-start.1 = (f32[256]{0:T(256)S(1)}, f32[256]{0:T(256)}, u32[]{:S(2)}) copy-start(f32[256]{0:T(256)} %param.10) | copy-start | bytes 3076
  99.1 32.7 %copy-start.2 = (f32[256]{0:T(256)S(1)}, f32[256]{0:T(256)}, u32[]{:S(2)}) copy-start(f32[256]{0:T(256)} %param.11) | copy-start | bytes 3076
  99.1 14.8 %collective-permute-start.5 = (f32[512,256]{0,1:T(8,128)S(1)}, f32[512,256]{0,1:T(8,128)S(1)}, u32[]{:S(2)}, u32[]{:S(2)}) collective-permute-start(f32[512,256]{0,1:T(8,128)S(1)} %fusion.2), channel_id=1, source_target_pairs={{0,1},{1,0},{2,3},{3,2},{4,5},{5,4},{6,7},{7,6},{8,9},{9,8},{10,11... | collective-permute-start | bytes 1572872 | tf_op jit(solution)/shard_map/ppermute | solution.py:66
Sparse Core Ops, SparseCore 0:
  22.1 57.7 all-gather.1

commit v9 on v8

--- a/solution.py
+++ b/solution.py
@@ -37,16 +37,10 @@
         jnp.concatenate([other_second, other_first], axis=1),
     )
     yl = lax.axis_index("yl")
-    piece = jnp.where(
-        yl == 0,
-        jnp.concatenate([own_block, other_block], axis=0),
-        jnp.concatenate([other_block, own_block], axis=0),
-    )
+    piece = jnp.where(yl == 0, jnp.stack([own_block, other_block]), jnp.stack([other_block, own_block]))
     second_x = lax.ppermute(dist_second, "zh", [(0, 1), (1, 0)])
 
-    gathered = lax.all_gather(piece, ("x", "zl", "core"), axis=0, tiled=True)
-    gathered = gathered.reshape(4, 2, 2, 2, blocks, 2 * k_half)
-    gathered = jnp.transpose(gathered, (3, 0, 1, 2, 4, 5)).reshape(-1, 2 * k_half)
+    gathered = lax.all_gather(piece, ("x", "zl", "core"), axis=1, tiled=True).reshape(-1, 2 * k_half)
 
     second_full = jnp.concatenate([dist_second, second_x], axis=1)
     second_k = jnp.concatenate(

time: 140 us -> 134 us (0.957)
  local copies, waits for them, and re-layouts: 9.36 us -> 1.88 us
  starting transfers between devices: 18.9 us -> 20.5 us
    transpose x1 -> x0, local copies, waits for them, and re-layouts: 7.47 us -> none  [body(): jnp.transpose(gathered, (3, 0, 1, 2, 4, 5)).reshape(-1, 2 * k_half)]
    ppermute x1, starting transfers between devices: 4.5 us -> 10.5 us  [body(): lax.ppermute(coupling, ('yh', 'zh'), [(1, 0), (2, 3), (0, 2), (3, 1)])]
    ppermute x1, starting transfers between devices: 7.3 us -> 2.98 us  [body(): second_x = lax.ppermute(dist_second, 'zh', [(0, 1), (1, 0)])]
    ppermute x1, waiting for transfers between devices: 3.66 us -> 2.16 us  [body(): lax.ppermute(coupling, ('yh', 'zh'), [(1, 0), (2, 3), (0, 2), (3, 1)])]
  transfers between devices with their start and end apart: 7 -> 7, of which waited for: 5 -> 4; matrix products, arithmetic and copies ran while one was open for 9% -> 10% of each run, Pallas kernels for 0% -> 0%
where the time goes in v9:
time: 134 us; the launch traced here: 133 us
  waiting for transfers between devices  53 us (40%)
  matrix products  23.4 us (17%)
  starting transfers between devices  20.5 us (15%)
  blocking collectives  17.1 us (13%)
  between operations  14.1 us (11%)
  other arithmetic  3.34 us (2%)
  local copies, waits for them, and re-layouts  1.88 us (1%)
    all_gather x1, waiting for transfers between devices, body(): lax.all_gather(piece, ('x', 'zl', 'core'), axis=1, tiled=True)  48.8 us
    dot_general x2, matrix products, partial_gradient(): return jnp.dot(dist_first, product, preferred_element_type=jnp.float32)  23.4 us
    all_to_all x1, blocking collectives, body(): pairs = lax.all_to_all(copies, ROWS, 0, 0, tiled=True)  17.1 us
    ppermute x1, starting transfers between devices, body(): lax.ppermute(coupling, ('yh', 'zh'), [(1, 0), (2, 3), (0, 2), (3, 1)])  10.5 us
    ppermute x1, starting transfers between devices, body(): other_second = lax.ppermute(coupling, ('yh', 'yl', 'zh'), second_pairs)  3.63 us
    ppermute x1, starting transfers between devices, body(): second_x = lax.ppermute(dist_second, 'zh', [(0, 1), (1, 0)])  2.98 us
    ppermute x1, starting transfers between devices, body(): arrived = lax.ppermute(other_part, 'zh', [(0, 1), (1, 0)])  2.78 us
  transfers between devices with their start and end apart: 7, of which 4 were waited for; matrix products, arithmetic and copies ran while one was open for 10% of the time, Pallas kernels for 0%

profile of v9, /device:TPU:1, one launch (start us, length us, event | category | flops | bytes accessed | tf_op | source)
XLA Modules:
  0.0 133.4 jit_solution(17656295155294586790)
XLA Ops:
  7.2 0.0 all-gather.2.cloned.1.call-start
  7.2 3.6 %collective-permute-start.3 = (bf16[512,128]{1,0:T(8,128)(2,1)}, bf16[512,128]{1,0:T(8,128)(2,1)S(1)}, u32[]{:S(2)}, u32[]{:S(2)}) collective-permute-start(bf16[512,128]{1,0:T(8,128)(2,1)} %param.7), channel_id=1, source_target_pairs={{0,96},{1,32},{32,64},{33,0},{65,33},{64,97},{97,1},{96,65},{2,98}... | collective-permute-start | bytes 393224 | tf_op jit(solution)/shard_map/ppermute | solution.py:31
  10.8 0.0 collective-permute-start.2
  10.8 0.7 collective-permute-start.1
  11.5 10.5 %collective-permute-start = (bf16[512,128]{1,0:T(8,128)(2,1)}, bf16[512,128]{1,0:T(8,128)(2,1)S(1)}, u32[]{:S(2)}, u32[]{:S(2)}) collective-permute-start(bf16[512,128]{1,0:T(8,128)(2,1)} %param.7), channel_id=1, source_target_pairs={{1,0},{64,65},{0,64},{65,1},{3,2},{66,67},{2,66},{67,3},{5,4},{68,... | collective-permute-start | bytes 393224 | tf_op jit(solution)/shard_map/ppermute | solution.py:20
  22.0 0.0 collective-permute-done.3
  22.0 0.0 collective-permute-done.2
  22.0 0.1 maximum_select_fusion.2
  22.1 0.0 collective-permute-done.1
  22.1 2.2 %collective-permute-done = bf16[512,128]{1,0:T(8,128)(2,1)S(1)} collective-permute-done((bf16[512,128]{1,0:T(8,128)(2,1)}, bf16[512,128]{1,0:T(8,128)(2,1)S(1)}, u32[]{:S(2)}, u32[]{:S(2)}) %collective-permute-start) | collective-permute-done | bytes 131104 | tf_op jit(solution)/shard_map/ppermute | solution.py:20
  24.2 1.0 maximum_select_fusion.1
  25.2 0.9 maximum_select_fusion
  26.1 0.0 all-gather.2.cloned.1.call-update
  26.2 3.0 %collective-permute-start.4 = (bf16[256,256]{1,0:T(8,128)(2,1)}, bf16[256,256]{1,0:T(8,128)(2,1)S(1)}, u32[]{:S(2)}, u32[]{:S(2)}) collective-permute-start(bf16[256,256]{1,0:T(8,128)(2,1)} %param.8), channel_id=1, source_target_pairs={{0,1},{1,0},{2,3},{3,2},{4,5},{5,4},{6,7},{7,6},{8,9},{9,8},{10,11... | collective-permute-start | bytes 393224 | tf_op jit(solution)/shard_map/ppermute | solution.py:41
  29.1 0.9 constant_dynamic-update-slice_fusion.1
  30.1 1.7 %collective-permute-done.4 = bf16[256,256]{1,0:T(8,128)(2,1)S(1)} collective-permute-done((bf16[256,256]{1,0:T(8,128)(2,1)}, bf16[256,256]{1,0:T(8,128)(2,1)S(1)}, u32[]{:S(2)}, u32[]{:S(2)}) %collective-permute-start.4) | collective-permute-done | bytes 131104 | tf_op jit(solution)/shard_map/ppermute | solution.py:41
  31.8 48.8 %all-gather.2.cloned.1.call-done = bf16[2,8192,256]{2,1,0:T(8,128)(2,1)} async-done(((bf16[2,512,256]{2,1,0:T(8,128)(2,1)}), bf16[2,8192,256]{2,1,0:T(8,128)(2,1)}) %all-gather.2.cloned.1.call-update) | async-done | bytes 8388624 | tf_op jit(solution)/shard_map/all_gather | solution.py:43
  80.6 11.7 %fusion.2 = f32[512,256]{0,1:T(8,128)S(1)} fusion(bf16[512,16384]{1,0:T(8,128)(2,1)} %param.6, bf16[16384,256]{1,0:T(8,128)(2,1)} %bitcast.35, bf16[128,512]{1,0:T(8,128)(2,1)S(1)} %get-tuple-element.14, bf16[128,512]{1,0:T(8,128)(2,1)S(1)} %get-tuple-element.15), kind=kOutput, calls=%fused_computation.4 | convolution fusion | flops 6446907392 | bytes 25952256 | tf_op jit(solution)/shard_map/dot_general | solution.py:57
  92.3 0.0 copy-start
  92.3 0.0 copy-start.1
  92.3 0.0 copy-start.2
  92.3 2.8 %collective-permute-start.5 = (f32[512,256]{0,1:T(8,128)S(1)}, f32[512,256]{0,1:T(8,128)S(1)}, u32[]{:S(2)}, u32[]{:S(2)}) collective-permute-start(f32[512,256]{0,1:T(8,128)S(1)} %fusion.2), channel_id=1, source_target_pairs={{0,1},{1,0},{2,3},{3,2},{4,5},{5,4},{6,7},{7,6},{8,9},{9,8},{10,11... | collective-permute-start | bytes 1572872 | tf_op jit(solution)/shard_map/ppermute | solution.py:60
  95.1 11.7 %fusion.3 = f32[512,256]{0,1:T(8,128)S(1)} fusion(bf16[512,16384]{1,0:T(8,128)(2,1)} %param.6, bf16[16384,256]{1,0:T(8,128)(2,1)} %bitcast.36, bf16[128,512]{1,0:T(8,128)(2,1)S(1)} %get-tuple-element.15, bf16[128,512]{1,0:T(8,128)(2,1)S(1)} %get-tuple-element.14), kind=kOutput, calls=%fused_computation.5 | convolution fusion | flops 6446907392 | bytes 25952256 | tf_op jit(solution)/shard_map/dot_general | solution.py:57
  106.8 0.4 collective-permute-done.5
  107.2 0.0 copy-done
  107.2 0.2 fusion.17
  107.4 0.2 exponential_reduce_fusion
  107.7 17.1 %all_to_all.5 = f32[64,2,256]{2,1,0:T(2,128)S(1)} all-to-all(f32[64,2,256]{2,1,0:T(2,128)S(1)} %broadcast_in_dim.2), channel_id=1, replica_groups=mesh['yh'=2,'yl'=2,'x'=4,'zl'=2,'core'=2,'zh'=2] {'yh','yl','x','zl','co..., dimensions={0} | all-to-all | bytes 262144 | tf_op jit(solution)/shard_map/all_to_all | solution.py:71
  124.8 0.1 slice_reduce_fusion
  125.0 0.6 log_subtract_fusion
  125.6 0.1 multiply_convert_fusion
  125.7 0.8 copy.12
  (7 shorter events, 0.1 us)
Async XLA Ops:
  7.2 73.4 %all-gather.2.cloned.1.call-start = ((), (), s32[]{:S(2)}) async-start(), calls=%async_computation.1 | async-start | bytes 8912896 | tf_op jit(solution)/shard_map/all_gather | solution.py:43
  7.2 14.8 %collective-permute-start.3 = (bf16[512,128]{1,0:T(8,128)(2,1)}, bf16[512,128]{1,0:T(8,128)(2,1)S(1)}, u32[]{:S(2)}, u32[]{:S(2)}) collective-permute-start(bf16[512,128]{1,0:T(8,128)(2,1)} %param.7), channel_id=1, source_target_pairs={{0,96},{1,32},{32,64},{33,0},{65,33},{64,97},{97,1},{96,65},{2,98}... | collective-permute-start | bytes 393224 | tf_op jit(solution)/shard_map/ppermute | solution.py:31
  10.8 11.1 %collective-permute-start.2 = (bf16[512,128]{1,0:T(8,128)(2,1)}, bf16[512,128]{1,0:T(8,128)(2,1)S(1)}, u32[]{:S(2)}, u32[]{:S(2)}) collective-permute-start(bf16[512,128]{1,0:T(8,128)(2,1)} %param.7), channel_id=1, source_target_pairs={{0,32},{1,96},{32,0},{33,64},{65,97},{64,33},{97,65},{96,1},{2,34}... | collective-permute-start | bytes 393224 | tf_op jit(solution)/shard_map/ppermute | solution.py:30
  10.8 11.2 %collective-permute-start.1 = (bf16[512,128]{1,0:T(8,128)(2,1)}, bf16[512,128]{1,0:T(8,128)(2,1)S(1)}, u32[]{:S(2)}, u32[]{:S(2)}) collective-permute-start(bf16[512,128]{1,0:T(8,128)(2,1)} %param.7), channel_id=1, source_target_pairs={{1,64},{64,1},{3,66},{66,3},{5,68},{68,5},{7,70},{70,7},{9,72},{72... | collective-permute-start | bytes 393224 | tf_op jit(solution)/shard_map/ppermute | solution.py:21
  11.5 12.7 %collective-permute-start = (bf16[512,128]{1,0:T(8,128)(2,1)}, bf16[512,128]{1,0:T(8,128)(2,1)S(1)}, u32[]{:S(2)}, u32[]{:S(2)}) collective-permute-start(bf16[512,128]{1,0:T(8,128)(2,1)} %param.7), channel_id=1, source_target_pairs={{1,0},{64,65},{0,64},{65,1},{3,2},{66,67},{2,66},{67,3},{5,4},{68,... | collective-permute-start | bytes 393224 | tf_op jit(solution)/shard_map/ppermute | solution.py:20
  26.2 5.6 %collective-permute-start.4 = (bf16[256,256]{1,0:T(8,128)(2,1)}, bf16[256,256]{1,0:T(8,128)(2,1)S(1)}, u32[]{:S(2)}, u32[]{:S(2)}) collective-permute-start(bf16[256,256]{1,0:T(8,128)(2,1)} %param.8), channel_id=1, source_target_pairs={{0,1},{1,0},{2,3},{3,2},{4,5},{5,4},{6,7},{7,6},{8,9},{9,8},{10,11... | collective-permute-start | bytes 393224 | tf_op jit(solution)/shard_map/ppermute | solution.py:41
  92.3 14.9 %copy-start = (f32[512]{0:T(512)S(1)}, f32[512]{0:T(512)}, u32[]{:S(2)}) copy-start(f32[512]{0:T(512)} %param.9) | copy-start | bytes 6148
  92.3 14.9 %copy-start.1 = (f32[256]{0:T(256)S(1)}, f32[256]{0:T(256)}, u32[]{:S(2)}) copy-start(f32[256]{0:T(256)} %param.10) | copy-start | bytes 3076
  92.3 32.7 %copy-start.2 = (f32[256]{0:T(256)S(1)}, f32[256]{0:T(256)}, u32[]{:S(2)}) copy-start(f32[256]{0:T(256)} %param.11) | copy-start | bytes 3076
  92.3 14.9 %collective-permute-start.5 = (f32[512,256]{0,1:T(8,128)S(1)}, f32[512,256]{0,1:T(8,128)S(1)}, u32[]{:S(2)}, u32[]{:S(2)}) collective-permute-start(f32[512,256]{0,1:T(8,128)S(1)} %fusion.2), channel_id=1, source_target_pairs={{0,1},{1,0},{2,3},{3,2},{4,5},{5,4},{6,7},{7,6},{8,9},{9,8},{10,11... | collective-permute-start | bytes 1572872 | tf_op jit(solution)/shard_map/ppermute | solution.py:60
Sparse Core Ops, SparseCore 0:
  26.3 54.2 all-gather.1

commit v10 on v4

--- a/solution.py
+++ b/solution.py
@@ -8,7 +8,6 @@
 N = 32768
 AXES = ("yh", "yl", "x", "zl", "core", "zh")
 ROWS = ("yh", "yl", "x", "zl", "core")
-GATHER = ("yl", "x", "zl", "core")
 
 
 def body(dist_first, coupling, dist_second, row_potential, column_cost, column_mass):
@@ -18,13 +17,21 @@
     k_half = coupling.shape[1]
     q_half = dist_second.shape[1]
 
-    near = lax.ppermute(coupling, ("yh", "zh"), [(1, 0), (2, 3), (0, 2), (3, 1)])
-    far = lax.ppermute(coupling, ("yh", "zh"), [(1, 2), (2, 1)])
-    holds = yh == zh
-    piece = jnp.where(holds, jnp.concatenate([coupling, near], axis=1), jnp.concatenate([near, far], axis=1))
+    column = lax.axis_size("yh") * lax.axis_size("yl") * lax.axis_size("zh")
+    copies = jnp.broadcast_to(coupling, (column, *coupling.shape))
+    column_blocks = lax.all_to_all(copies, ("yh", "yl", "zh"), 0, 0, tiled=True)
+    column_blocks = column_blocks.reshape(2, 2, 2, blocks, k_half)
+    mine = lax.dynamic_index_in_dim(column_blocks, zh, axis=0, keepdims=False)
+    piece = jnp.concatenate(
+        [
+            lax.dynamic_index_in_dim(mine, zh, axis=1, keepdims=False),
+            lax.dynamic_index_in_dim(mine, 1 - zh, axis=1, keepdims=False),
+        ],
+        axis=2,
+    )
     second_x = lax.ppermute(dist_second, "zh", [(0, 1), (1, 0)])
 
-    gathered = lax.all_gather(piece, GATHER, axis=0, tiled=True)
+    gathered = lax.all_gather(piece, ("x", "zl", "core"), axis=1, tiled=True).reshape(-1, 2 * k_half)
 
     second_full = jnp.concatenate([dist_second, second_x], axis=1)
     second_k = jnp.concatenate(

time: 142 us -> 139 us (0.979)
  waiting for transfers between devices: 69.8 us -> 65.4 us
  local copies, waits for them, and re-layouts: 1.88 us -> 3.93 us
  starting transfers between devices: 14.2 us -> 12.7 us
    all_gather x1, waiting for transfers between devices: 64 us -> 46.5 us  [body(): lax.all_gather(piece, ('x', 'zl', 'core'), axis=1, tiled=True)]
    all_to_all x0 -> x1, waiting for transfers between devices: none -> 15.4 us  [body(): column_blocks = lax.all_to_all(copies, ('yh', 'yl', 'zh'), 0, 0, tiled=True)]
    all_to_all x0 -> x1, starting transfers between devices: none -> 8.33 us  [body(): column_blocks = lax.all_to_all(copies, ('yh', 'yl', 'zh'), 0, 0, tiled=True)]
    ppermute x1, starting transfers between devices: 7.25 us -> 1.56 us  [body(): second_x = lax.ppermute(dist_second, 'zh', [(0, 1), (1, 0)])]
    ppermute x2 -> x0, starting transfers between devices: 4.47 us -> none  [the longest x1 3.81 us: body(): lax.ppermute(coupling, ('yh', 'zh'), [(1, 0), (2, 3), (0, 2), (3, 1)])]
    ppermute x2 -> x0, waiting for transfers between devices: 3.45 us -> none  [the longest x1 3.44 us: body(): lax.ppermute(coupling, ('yh', 'zh'), [(1, 0), (2, 3), (0, 2), (3, 1)])]
    broadcast_in_dim x0 -> x1, local copies, waits for them, and re-layouts: none -> 2.01 us  [body(): copies = jnp.broadcast_to(coupling, (column, *coupling.shape))]
    select_n x1 -> x0, other arithmetic: 1.68 us -> none  [body(): jnp.where(holds, jnp.concatenate([coupling, near], axis=1), jnp.concatena...]
  transfers between devices with their start and end apart: 5 -> 4, of which waited for: 4 -> 4; matrix products, arithmetic and copies ran while one was open for 9% -> 9% of each run, Pallas kernels for 0% -> 0%
where the time goes in v10:
time: 139 us
  waiting for transfers between devices  65.4 us (47%)
  matrix products  23.4 us (17%)
  blocking collectives  17.1 us (12%)
  between operations  14.1 us (10%)
  starting transfers between devices  12.7 us (9%)
  local copies, waits for them, and re-layouts  3.93 us (3%)
  other arithmetic  2.24 us (2%)
    all_gather x1, waiting for transfers between devices, body(): lax.all_gather(piece, ('x', 'zl', 'core'), axis=1, tiled=True)  46.5 us
    dot_general x2, matrix products, partial_gradient(): return jnp.dot(dist_first, product, preferred_element_type=jnp.float32)  23.4 us
    all_to_all x1, blocking collectives, body(): pairs = lax.all_to_all(copies, ROWS, 0, 0, tiled=True)  17.1 us
    all_to_all x1, waiting for transfers between devices, body(): column_blocks = lax.all_to_all(copies, ('yh', 'yl', 'zh'), 0, 0, tiled=True)  15.4 us
    all_to_all x1, starting transfers between devices, body(): column_blocks = lax.all_to_all(copies, ('yh', 'yl', 'zh'), 0, 0, tiled=True)  8.33 us
    ppermute x1, waiting for transfers between devices, body(): second_x = lax.ppermute(dist_second, 'zh', [(0, 1), (1, 0)])  3.11 us
  transfers between devices with their start and end apart: 4, of which 4 were waited for; matrix products, arithmetic and copies ran while one was open for 9% of the time, Pallas kernels for 0%

profile of v10, /device:TPU:1, one launch (start us, length us, event | category | flops | bytes accessed | tf_op | source)
XLA Modules:
  0.0 138.9 jit_solution(4511101953981956098)
XLA Ops:
  7.2 2.0 %broadcast_in_dim.4 = bf16[8,512,128]{2,1,0:T(8,128)(2,1)} broadcast(bf16[512,128]{1,0:T(8,128)(2,1)} %param.7), dimensions={1,2} | broadcast | bytes 1179648 | tf_op jit(solution)/shard_map/broadcast_in_dim | solution.py:21
  9.2 8.3 %all-to-all-start = ((bf16[8,512,128]{2,1,0:T(8,128)(2,1)}), bf16[8,512,128]{2,1,0:T(8,128)(2,1)S(1)}, u32[]{:S(2)}, u32[]{:S(2)}) async-start(bf16[8,512,128]{2,1,0:T(8,128)(2,1)} %broadcast_in_dim.4), calls=%async_computation | async-start | bytes 2097152 | tf_op jit(solution)/shard_map/all_to_all | solution.py:22
  17.5 0.0 all-gather.2.cloned.1.call-start
  17.6 15.4 %all-to-all-done = bf16[8,512,128]{2,1,0:T(8,128)(2,1)S(1)} async-done(((bf16[8,512,128]{2,1,0:T(8,128)(2,1)}), bf16[8,512,128]{2,1,0:T(8,128)(2,1)S(1)}, u32[]{:S(2)}, u32[]{:S(2)}) %all-to-all-start) | async-done | bytes 1048608 | tf_op jit(solution)/shard_map/all_to_all | solution.py:22
  33.0 0.9 pad_maximum_fusion
  33.9 0.0 all-gather.2.cloned.1.call-update
  33.9 1.6 %collective-permute-start = (bf16[256,256]{1,0:T(8,128)(2,1)}, bf16[256,256]{1,0:T(8,128)(2,1)S(1)}, u32[]{:S(2)}, u32[]{:S(2)}) collective-permute-start(bf16[256,256]{1,0:T(8,128)(2,1)} %param.8), channel_id=1, source_target_pairs={{0,1},{1,0},{2,3},{3,2},{4,5},{5,4},{6,7},{7,6},{8,9},{9,8},{10,11... | collective-permute-start | bytes 393224 | tf_op jit(solution)/shard_map/ppermute | solution.py:32
  35.5 0.9 constant_dynamic-update-slice_fusion.1
  36.5 3.1 %collective-permute-done = bf16[256,256]{1,0:T(8,128)(2,1)S(1)} collective-permute-done((bf16[256,256]{1,0:T(8,128)(2,1)}, bf16[256,256]{1,0:T(8,128)(2,1)S(1)}, u32[]{:S(2)}, u32[]{:S(2)}) %collective-permute-start) | collective-permute-done | bytes 131104 | tf_op jit(solution)/shard_map/ppermute | solution.py:32
  39.6 46.5 %all-gather.2.cloned.1.call-done = bf16[2,8192,256]{2,1,0:T(8,128)(2,1)} async-done(((bf16[2,512,256]{2,1,0:T(8,128)(2,1)}), bf16[2,8192,256]{2,1,0:T(8,128)(2,1)}) %all-gather.2.cloned.1.call-update) | async-done | bytes 8388624 | tf_op jit(solution)/shard_map/all_gather | solution.py:34
  86.1 11.7 %fusion.2 = f32[512,256]{0,1:T(8,128)S(1)} fusion(bf16[512,16384]{1,0:T(8,128)(2,1)} %param.6, bf16[16384,256]{1,0:T(8,128)(2,1)} %bitcast.31, bf16[128,512]{1,0:T(8,128)(2,1)S(1)} %get-tuple-element.16, bf16[128,512]{1,0:T(8,128)(2,1)S(1)} %get-tuple-element.17), kind=kOutput, calls=%fused_computation.4 | convolution fusion | flops 6446907392 | bytes 25952256 | tf_op jit(solution)/shard_map/dot_general | solution.py:48
  97.8 0.0 copy-start
  97.8 0.0 copy-start.1
  97.8 0.0 copy-start.2
  97.8 2.8 %collective-permute-start.1 = (f32[512,256]{0,1:T(8,128)S(1)}, f32[512,256]{0,1:T(8,128)S(1)}, u32[]{:S(2)}, u32[]{:S(2)}) collective-permute-start(f32[512,256]{0,1:T(8,128)S(1)} %fusion.2), channel_id=1, source_target_pairs={{0,1},{1,0},{2,3},{3,2},{4,5},{5,4},{6,7},{7,6},{8,9},{9,8},{10,11... | collective-permute-start | bytes 1572872 | tf_op jit(solution)/shard_map/ppermute | solution.py:51
  100.6 11.7 %fusion.3 = f32[512,256]{0,1:T(8,128)S(1)} fusion(bf16[512,16384]{1,0:T(8,128)(2,1)} %param.6, bf16[16384,256]{1,0:T(8,128)(2,1)} %bitcast.32, bf16[128,512]{1,0:T(8,128)(2,1)S(1)} %get-tuple-element.17, bf16[128,512]{1,0:T(8,128)(2,1)S(1)} %get-tuple-element.16), kind=kOutput, calls=%fused_computation.5 | convolution fusion | flops 6446907392 | bytes 25952256 | tf_op jit(solution)/shard_map/dot_general | solution.py:48
  112.3 0.4 collective-permute-done.1
  112.7 0.0 copy-done
  112.7 0.0 copy-done.1
  112.7 0.2 fusion.17
  112.9 0.2 exponential_reduce_fusion
  113.1 17.1 %all_to_all.10 = f32[64,2,256]{2,1,0:T(2,128)S(1)} all-to-all(f32[64,2,256]{2,1,0:T(2,128)S(1)} %broadcast_in_dim.5), channel_id=1, replica_groups=mesh['yh'=2,'yl'=2,'x'=4,'zl'=2,'core'=2,'zh'=2] {'yh','yl','x','zl','co..., dimensions={0} | all-to-all | bytes 262144 | tf_op jit(solution)/shard_map/all_to_all | solution.py:62
  130.2 0.1 slice_reduce_fusion
  130.4 0.0 copy-done.2
  130.4 0.6 log_subtract_fusion
  131.0 0.1 multiply_convert_fusion
  131.2 0.8 copy.12
  (6 shorter events, 0.2 us)
Async XLA Ops:
  9.2 23.8 %all-to-all-start = ((bf16[8,512,128]{2,1,0:T(8,128)(2,1)}), bf16[8,512,128]{2,1,0:T(8,128)(2,1)S(1)}, u32[]{:S(2)}, u32[]{:S(2)}) async-start(bf16[8,512,128]{2,1,0:T(8,128)(2,1)} %broadcast_in_dim.4), calls=%async_computation | async-start | bytes 2097152 | tf_op jit(solution)/shard_map/all_to_all | solution.py:22
  17.5 68.6 %all-gather.2.cloned.1.call-start = ((), (), s32[]{:S(2)}) async-start(), calls=%async_computation.2 | async-start | bytes 8912896 | tf_op jit(solution)/shard_map/all_gather | solution.py:34
  33.9 5.6 %collective-permute-start = (bf16[256,256]{1,0:T(8,128)(2,1)}, bf16[256,256]{1,0:T(8,128)(2,1)S(1)}, u32[]{:S(2)}, u32[]{:S(2)}) collective-permute-start(bf16[256,256]{1,0:T(8,128)(2,1)} %param.8), channel_id=1, source_target_pairs={{0,1},{1,0},{2,3},{3,2},{4,5},{5,4},{6,7},{7,6},{8,9},{9,8},{10,11... | collective-permute-start | bytes 393224 | tf_op jit(solution)/shard_map/ppermute | solution.py:32
  97.8 14.9 %copy-start = (f32[512]{0:T(512)S(1)}, f32[512]{0:T(512)}, u32[]{:S(2)}) copy-start(f32[512]{0:T(512)} %param.9) | copy-start | bytes 6148
  97.8 14.9 %copy-start.1 = (f32[256]{0:T(256)S(1)}, f32[256]{0:T(256)}, u32[]{:S(2)}) copy-start(f32[256]{0:T(256)} %param.10) | copy-start | bytes 3076
  97.8 32.7 %copy-start.2 = (f32[256]{0:T(256)S(1)}, f32[256]{0:T(256)}, u32[]{:S(2)}) copy-start(f32[256]{0:T(256)} %param.11) | copy-start | bytes 3076
  97.8 14.9 %collective-permute-start.1 = (f32[512,256]{0,1:T(8,128)S(1)}, f32[512,256]{0,1:T(8,128)S(1)}, u32[]{:S(2)}, u32[]{:S(2)}) collective-permute-start(f32[512,256]{0,1:T(8,128)S(1)} %fusion.2), channel_id=1, source_target_pairs={{0,1},{1,0},{2,3},{3,2},{4,5},{5,4},{6,7},{7,6},{8,9},{9,8},{10,11... | collective-permute-start | bytes 1572872 | tf_op jit(solution)/shard_map/ppermute | solution.py:51
Sparse Core Ops, SparseCore 0:
  34.1 51.9 all-gather.1

commit v11 on v9

--- a/solution.py
+++ b/solution.py
@@ -2,6 +2,7 @@
 import jax.numpy as jnp
 import numpy as np
 from jax import lax
+from jax.experimental.layout import Layout, with_layout_constraint
 from jax.sharding import Mesh
 from jax.sharding import PartitionSpec as P
 
@@ -54,7 +55,8 @@
         product = jnp.dot(
             gathered, second_k[:, cols], preferred_element_type=jnp.float32
         ).astype(jnp.bfloat16)
-        return jnp.dot(dist_first, product, preferred_element_type=jnp.float32)
+        part = jnp.dot(dist_first, product, preferred_element_type=jnp.float32)
+        return with_layout_constraint(part, Layout((0, 1)))
 
     other_part = partial_gradient(slice(q_half, 2 * q_half))
     arrived = lax.ppermute(other_part, "zh", [(0, 1), (1, 0)])

time: 134 us -> 141 us (1.052)
  matrix products: 23.4 us -> 32.1 us
    dot_general x2, matrix products: 23.4 us -> 32.1 us  [partial_gradient(): part = jnp.dot(dist_first, product, preferred_element_type=jnp.float32)]
  transfers between devices with their start and end apart: 7 -> 7, of which waited for: 4 -> 3; matrix products, arithmetic and copies ran while one was open for 10% -> 12% of each run, Pallas kernels for 0% -> 0%
where the time goes in v11:
time: 141 us; the launch traced here: 140 us
  waiting for transfers between devices  52.6 us (37%)
  matrix products  32.1 us (23%)
  starting transfers between devices  20.7 us (15%)
  blocking collectives  15.9 us (11%)
  between operations  14.1 us (10%)
  other arithmetic  3.87 us (3%)
    all_gather x1, waiting for transfers between devices, body(): lax.all_gather(piece, ('x', 'zl', 'core'), axis=1, tiled=True)  48.8 us
    dot_general x2, matrix products, partial_gradient(): part = jnp.dot(dist_first, product, preferred_element_type=jnp.float32)  32.1 us
    all_to_all x1, blocking collectives, body(): pairs = lax.all_to_all(copies, ROWS, 0, 0, tiled=True)  15.9 us
    ppermute x1, starting transfers between devices, body(): lax.ppermute(coupling, ('yh', 'zh'), [(1, 0), (2, 3), (0, 2), (3, 1)])  10.5 us
    ppermute x1, starting transfers between devices, body(): other_second = lax.ppermute(coupling, ('yh', 'yl', 'zh'), second_pairs)  3.63 us
    ppermute x1, starting transfers between devices, body(): second_x = lax.ppermute(dist_second, 'zh', [(0, 1), (1, 0)])  2.98 us
    ppermute x1, starting transfers between devices, body(): arrived = lax.ppermute(other_part, 'zh', [(0, 1), (1, 0)])  2.96 us
  transfers between devices with their start and end apart: 7, of which 3 were waited for; matrix products, arithmetic and copies ran while one was open for 12% of the time, Pallas kernels for 0%

profile of v11, /device:TPU:1, one launch (start us, length us, event | category | flops | bytes accessed | tf_op | source)
XLA Modules:
  0.0 140.4 jit_solution(9184961119729041990)
XLA Ops:
  7.2 0.0 all-gather.2.cloned.1.call-start
  7.2 3.6 %collective-permute-start.3 = (bf16[512,128]{1,0:T(8,128)(2,1)}, bf16[512,128]{1,0:T(8,128)(2,1)S(1)}, u32[]{:S(2)}, u32[]{:S(2)}) collective-permute-start(bf16[512,128]{1,0:T(8,128)(2,1)} %param.7), channel_id=1, source_target_pairs={{0,96},{1,32},{32,64},{33,0},{65,33},{64,97},{97,1},{96,65},{2,98}... | collective-permute-start | bytes 393224 | tf_op jit(solution)/shard_map/ppermute | solution.py:32
  10.8 0.0 collective-permute-start.2
  10.8 0.7 collective-permute-start.1
  11.5 10.5 %collective-permute-start = (bf16[512,128]{1,0:T(8,128)(2,1)}, bf16[512,128]{1,0:T(8,128)(2,1)S(1)}, u32[]{:S(2)}, u32[]{:S(2)}) collective-permute-start(bf16[512,128]{1,0:T(8,128)(2,1)} %param.7), channel_id=1, source_target_pairs={{1,0},{64,65},{0,64},{65,1},{3,2},{66,67},{2,66},{67,3},{5,4},{68,... | collective-permute-start | bytes 393224 | tf_op jit(solution)/shard_map/ppermute | solution.py:21
  22.0 0.0 collective-permute-done.3
  22.0 0.0 collective-permute-done.2
  22.0 0.1 maximum_select_fusion.2
  22.1 0.0 collective-permute-done.1
  22.1 2.2 %collective-permute-done = bf16[512,128]{1,0:T(8,128)(2,1)S(1)} collective-permute-done((bf16[512,128]{1,0:T(8,128)(2,1)}, bf16[512,128]{1,0:T(8,128)(2,1)S(1)}, u32[]{:S(2)}, u32[]{:S(2)}) %collective-permute-start) | collective-permute-done | bytes 131104 | tf_op jit(solution)/shard_map/ppermute | solution.py:21
  24.2 1.0 maximum_select_fusion.1
  25.2 0.9 maximum_select_fusion
  26.1 0.0 all-gather.2.cloned.1.call-update
  26.2 3.0 %collective-permute-start.4 = (bf16[256,256]{1,0:T(8,128)(2,1)}, bf16[256,256]{1,0:T(8,128)(2,1)S(1)}, u32[]{:S(2)}, u32[]{:S(2)}) collective-permute-start(bf16[256,256]{1,0:T(8,128)(2,1)} %param.8), channel_id=1, source_target_pairs={{0,1},{1,0},{2,3},{3,2},{4,5},{5,4},{6,7},{7,6},{8,9},{9,8},{10,11... | collective-permute-start | bytes 393224 | tf_op jit(solution)/shard_map/ppermute | solution.py:42
  29.1 0.9 constant_dynamic-update-slice_fusion.1
  30.1 1.7 %collective-permute-done.4 = bf16[256,256]{1,0:T(8,128)(2,1)S(1)} collective-permute-done((bf16[256,256]{1,0:T(8,128)(2,1)}, bf16[256,256]{1,0:T(8,128)(2,1)S(1)}, u32[]{:S(2)}, u32[]{:S(2)}) %collective-permute-start.4) | collective-permute-done | bytes 131104 | tf_op jit(solution)/shard_map/ppermute | solution.py:42
  31.8 48.8 %all-gather.2.cloned.1.call-done = bf16[2,8192,256]{2,1,0:T(8,128)(2,1)} async-done(((bf16[2,512,256]{2,1,0:T(8,128)(2,1)}), bf16[2,8192,256]{2,1,0:T(8,128)(2,1)}) %all-gather.2.cloned.1.call-update) | async-done | bytes 8388624 | tf_op jit(solution)/shard_map/all_gather | solution.py:44
  80.6 16.0 %convolution_bitcast_fusion = f32[512,256]{1,0:T(8,128)S(1)} fusion(bf16[512,16384]{1,0:T(8,128)(2,1)} %param.6, bf16[16384,256]{1,0:T(8,128)(2,1)} %bitcast.35, bf16[128,512]{1,0:T(8,128)(2,1)S(1)} %get-tuple-element.8, bf16[128,512]{1,0:T(8,128)(2,1)S(1)} %get-tuple-element.9), kind=kOutput, calls=%fused_computation.2 | convolution fusion | flops 6446907392 | bytes 25952256 | tf_op jit(solution)/shard_map/dot_general | solution.py:58
  96.7 0.0 copy-start
  96.7 0.0 copy-start.1
  96.7 0.0 copy-start.2
  96.7 3.0 %collective-permute-start.5 = (f32[512,256]{1,0:T(8,128)S(1)}, f32[512,256]{1,0:T(8,128)S(1)}, u32[]{:S(2)}, u32[]{:S(2)}) collective-permute-start(f32[512,256]{1,0:T(8,128)S(1)} %convolution_bitcast_fusion), channel_id=1, source_target_pairs={{0,1},{1,0},{2,3},{3,2},{4,5},{5,4},{6,7},{7,6},{8,9},{9,8},{10,11... | collective-permute-start | bytes 1572872 | tf_op jit(solution)/shard_map/ppermute | solution.py:62
  99.7 16.0 %convolution_bitcast_fusion.1 = f32[512,256]{1,0:T(8,128)S(1)} fusion(bf16[512,16384]{1,0:T(8,128)(2,1)} %param.6, bf16[16384,256]{1,0:T(8,128)(2,1)} %bitcast.36, bf16[128,512]{1,0:T(8,128)(2,1)S(1)} %get-tuple-element.9, bf16[128,512]{1,0:T(8,128)(2,1)S(1)} %get-tuple-element.8), kind=kOutput, calls=%fused_computation.3 | convolution fusion | flops 6446907392 | bytes 25952256 | tf_op jit(solution)/shard_map/dot_general | solution.py:58
  115.7 0.0 collective-permute-done.5
  115.7 0.0 copy-done
  115.7 0.0 copy-done.1
  115.7 0.2 fusion.13
  115.9 0.1 exponential_reduce_fusion
  116.1 15.9 %all_to_all.5 = f32[64,2,256]{2,1,0:T(2,128)S(1)} all-to-all(f32[64,2,256]{2,1,0:T(2,128)S(1)} %broadcast_in_dim.2), channel_id=1, replica_groups=mesh['yh'=2,'yl'=2,'x'=4,'zl'=2,'core'=2,'zh'=2] {'yh','yl','x','zl','co..., dimensions={0} | all-to-all | bytes 262144 | tf_op jit(solution)/shard_map/all_to_all | solution.py:73
  132.0 0.1 slice_reduce_fusion
  132.2 0.6 log_subtract_fusion
  132.7 0.8 multiply_convert_fusion
  (6 shorter events, 0.1 us)
Async XLA Ops:
  7.2 73.4 %all-gather.2.cloned.1.call-start = ((), (), s32[]{:S(2)}) async-start(), calls=%async_computation.1 | async-start | bytes 8912896 | tf_op jit(solution)/shard_map/all_gather | solution.py:44
  7.2 14.8 %collective-permute-start.3 = (bf16[512,128]{1,0:T(8,128)(2,1)}, bf16[512,128]{1,0:T(8,128)(2,1)S(1)}, u32[]{:S(2)}, u32[]{:S(2)}) collective-permute-start(bf16[512,128]{1,0:T(8,128)(2,1)} %param.7), channel_id=1, source_target_pairs={{0,96},{1,32},{32,64},{33,0},{65,33},{64,97},{97,1},{96,65},{2,98}... | collective-permute-start | bytes 393224 | tf_op jit(solution)/shard_map/ppermute | solution.py:32
  10.8 11.1 %collective-permute-start.2 = (bf16[512,128]{1,0:T(8,128)(2,1)}, bf16[512,128]{1,0:T(8,128)(2,1)S(1)}, u32[]{:S(2)}, u32[]{:S(2)}) collective-permute-start(bf16[512,128]{1,0:T(8,128)(2,1)} %param.7), channel_id=1, source_target_pairs={{0,32},{1,96},{32,0},{33,64},{65,97},{64,33},{97,65},{96,1},{2,34}... | collective-permute-start | bytes 393224 | tf_op jit(solution)/shard_map/ppermute | solution.py:31
  10.8 11.2 %collective-permute-start.1 = (bf16[512,128]{1,0:T(8,128)(2,1)}, bf16[512,128]{1,0:T(8,128)(2,1)S(1)}, u32[]{:S(2)}, u32[]{:S(2)}) collective-permute-start(bf16[512,128]{1,0:T(8,128)(2,1)} %param.7), channel_id=1, source_target_pairs={{1,64},{64,1},{3,66},{66,3},{5,68},{68,5},{7,70},{70,7},{9,72},{72... | collective-permute-start | bytes 393224 | tf_op jit(solution)/shard_map/ppermute | solution.py:22
  11.5 12.7 %collective-permute-start = (bf16[512,128]{1,0:T(8,128)(2,1)}, bf16[512,128]{1,0:T(8,128)(2,1)S(1)}, u32[]{:S(2)}, u32[]{:S(2)}) collective-permute-start(bf16[512,128]{1,0:T(8,128)(2,1)} %param.7), channel_id=1, source_target_pairs={{1,0},{64,65},{0,64},{65,1},{3,2},{66,67},{2,66},{67,3},{5,4},{68,... | collective-permute-start | bytes 393224 | tf_op jit(solution)/shard_map/ppermute | solution.py:21
  26.2 5.6 %collective-permute-start.4 = (bf16[256,256]{1,0:T(8,128)(2,1)}, bf16[256,256]{1,0:T(8,128)(2,1)S(1)}, u32[]{:S(2)}, u32[]{:S(2)}) collective-permute-start(bf16[256,256]{1,0:T(8,128)(2,1)} %param.8), channel_id=1, source_target_pairs={{0,1},{1,0},{2,3},{3,2},{4,5},{5,4},{6,7},{7,6},{8,9},{9,8},{10,11... | collective-permute-start | bytes 393224 | tf_op jit(solution)/shard_map/ppermute | solution.py:42
  96.7 19.1 %copy-start = (f32[512]{0:T(512)S(1)}, f32[512]{0:T(512)}, u32[]{:S(2)}) copy-start(f32[512]{0:T(512)} %param.9) | copy-start | bytes 6148
  96.7 19.1 %copy-start.1 = (f32[256]{0:T(256)S(1)}, f32[256]{0:T(256)}, u32[]{:S(2)}) copy-start(f32[256]{0:T(256)} %param.10) | copy-start | bytes 3076
  96.7 35.5 %copy-start.2 = (f32[256]{0:T(256)S(1)}, f32[256]{0:T(256)}, u32[]{:S(2)}) copy-start(f32[256]{0:T(256)} %param.11) | copy-start | bytes 3076
  96.7 19.0 %collective-permute-start.5 = (f32[512,256]{1,0:T(8,128)S(1)}, f32[512,256]{1,0:T(8,128)S(1)}, u32[]{:S(2)}, u32[]{:S(2)}) collective-permute-start(f32[512,256]{1,0:T(8,128)S(1)} %convolution_bitcast_fusion), channel_id=1, source_target_pairs={{0,1},{1,0},{2,3},{3,2},{4,5},{5,4},{6,7},{7,6},{8,9},{9,8},{10,11... | collective-permute-start | bytes 1572872 | tf_op jit(solution)/shard_map/ppermute | solution.py:62
Sparse Core Ops, SparseCore 0:
  26.3 54.2 all-gather.1
